TPU v7x, 32 devices: a whole 2x2x4 slice. The times are simulated.
32 devices in a mesh: dp: 16 (over z, y, core), tensor: 2 (over x).
Axes of the slice: x: 2, y: 2, z: 4, core: 2. Of those that a mesh axis runs over, the one named last changes fastest.
Arguments:
- hidden_states: bfloat16 [8192, 2048], P('dp', 'tensor'), may hold values from -6 to 6
- norm_gain: bfloat16 [2048], replicated, may hold values from 0.25 to 1.75
- head_weight: bfloat16 [2048, 25600], P(None, ('tensor', 'dp')), may hold values from -1 to 1
- target_ids: int32 [8192], P('dp'), may hold values from 0 to 25599
- loss_mask: int32 [8192], P('dp'), may hold values from 0 to 1, as said below
- seq_lengths: int32 [16], replicated, may hold values from 1 to 4096, as said below
- slot_order: int32 [16], replicated, may hold values from 0 to 15, each once
Outputs:
- token_logprob: float32 [8192], P(('dp', 'tensor'))
- token_entropy: float32 [8192], P(('dp', 'tensor'))
- seq_mean_logprob: float32 [16], P('dp')
- seq_mean_entropy: float32 [16], P('dp')
Inputs may be any that keep to these rules, and one draw needn't show every extreme that they name: `seq_lengths`: sequences lie in packed order, one after another; their lengths sum to 8192; the longest has exactly 4096 tokens and some sequence has exactly 1 token. `slot_order`: each sequence appears once. `loss_mask`: some sequence of exactly 1 token has no scored row.
All inputs are finite; a program needn't handle non-finite values.
Results may differ from a plain program's by a relative error of at most 0.0012.
Values may be sent and summed in bfloat16 or wider, within the bound.
No kernel may reach another device: no remote copies, remote signals or barrier semaphores. Data moves between devices by JAX's collectives and lax.ppermute only.
A program may use at most 192 MiB of HBM per device.

v0:
```python
import jax
import jax.numpy as jnp
import numpy as np
from jax import lax
from jax.sharding import Mesh
from jax.sharding import PartitionSpec as P

EPS = 1e-05
ROWS = ("dh", "p", "dl")
ALL = ("dh", "p", "dl", "t")


def swap(x, name):
    return lax.ppermute(x, name, [(0, 1), (1, 0)])


def whole_rows(x, t, nt, other=None):
    if nt == 2:
        if other is None:
            other = swap(x, "t")
        return jnp.where(t == 0, jnp.concatenate([x, other], 1), jnp.concatenate([other, x], 1))
    return lax.all_gather(x, "t", axis=1, tiled=True)


def shifted(x, s, n, dh):
    if s == 0:
        return x
    if n <= 4:
        return lax.ppermute(x, "dh", [(i, (i + s) % n) for i in range(n)])
    return None


def per_device(hidden_states, norm_gain, head_weight, target_ids, loss_mask, seq_lengths, slot_order):
    rb, dt = hidden_states.shape
    nt = lax.axis_size("t")
    n = lax.axis_size("dh")
    nd = n * 4
    d = dt * nt
    cb = head_weight.shape[1]
    t = lax.axis_index("t")
    dh = lax.axis_index("dh")
    p = lax.axis_index("p")
    dl = lax.axis_index("dl")
    b = (dh * 2 + p) * 2 + dl

    w_p = swap(head_weight, "p")
    block_of = jnp.stack([b, (dh * 2 + 1 - p) * 2 + dl, (dh * 2 + p) * 2 + 1 - dl, (dh * 2 + 1 - p) * 2 + 1 - dl])
    column = ((t * nd + block_of)[:, None] * cb + jnp.arange(cb, dtype=jnp.int32)[None, :]).reshape(-1)

    gain = norm_gain.astype(jnp.float32)
    if n > 4:
        gathered_h = lax.all_gather(hidden_states, "dh", axis=0, tiled=False)
        gathered_t = lax.all_gather(target_ids, "dh", axis=0, tiled=False)

    else:
        fast = nt == 2 and (2 * rb) % dt == 0
        if not fast:
            moved = [shifted(hidden_states, s, n, dh) for s in range(1, n)]
            moved_t = [shifted(target_ids, s, n, dh) for s in range(1, n)]
            w_p, moved, moved_t = lax.optimization_barrier((w_p, moved, moved_t))

    def normalize(values):
        values = values.astype(jnp.float32)
        square = jnp.mean(values * values, axis=1, keepdims=True)
        return (values * lax.rsqrt(square + EPS) * gain[None, :]).astype(jnp.bfloat16)

    def block_stats(values, t_s, w_all, col=None):
        col = column if col is None else col
        logits = jnp.dot(normalize(values), w_all, preferred_element_type=jnp.float32)
        top = jnp.max(logits, axis=1)
        shift = logits - top[:, None]
        expo = jnp.exp(shift)
        total = jnp.sum(expo, axis=1)
        spread = jnp.sum(expo * shift, axis=1)
        picked = jnp.sum(jnp.where(col[None, :] == t_s[:, None], logits, 0.0), axis=1)
        return jnp.stack([top, total, spread, picked])

    def combine(pieces):
        got = jnp.stack(pieces)
        tops, totals, spreads, pickeds = got[:, 0], got[:, 1], got[:, 2], got[:, 3]
        top = jnp.max(tops, axis=0)
        scale = jnp.exp(tops - top[None, :])
        total = jnp.sum(totals * scale, axis=0)
        spread = jnp.sum(scale * (spreads + totals * (tops - top[None, :])), axis=0)
        return jnp.stack([top, total, spread, jnp.sum(pickeds, axis=0)])

    def joined(x, other):
        return jnp.where(t == 0, jnp.concatenate([x, other], 1), jnp.concatenate([other, x], 1))

    stats = []
    if n <= 4 and fast:
        extra = (2 * rb) // dt
        code = jnp.concatenate([target_ids // 128, target_ids % 128]).astype(jnp.bfloat16).reshape(extra, dt)
        carried = jnp.concatenate([hidden_states, code], 0)
        near = [s for s in sorted({1, n - 1}) if 1 <= s < n]
        far = [s for s in range(1, n) if s not in near]
        cols = [column[i * cb:(i + 1) * cb] for i in range(4)]

        def unpack(block):
            parts = block[rb:].reshape(2, rb).astype(jnp.int32)
            return block[:rb], parts[0] * 128 + parts[1]

        own_other, w_c, got = lax.optimization_barrier(
            (swap(hidden_states, "t"), swap(head_weight, "dl"), [shifted(carried, s, n, dh) for s in near]))
        rows = {0: (hidden_states, target_ids)}
        for s, block in zip(near, got):
            rows[s] = unpack(block)
        values = {0: joined(hidden_states, own_other)}
        w_own = jnp.concatenate([head_weight, w_c], 1)
        c_own = jnp.concatenate([cols[0], cols[2]])
        held = ((w_own, c_own), (w_p, cols[1]))
        first = [block_stats(values[0], target_ids, w, c) for w, c in held]
        first, got, others = lax.optimization_barrier(
            (first, [shifted(carried, s, n, dh) for s in far], [swap(rows[s][0], "t") for s in near]))
        for s, block in zip(far, got):
            rows[s] = unpack(block)
        for s, other in zip(near, others):
            values[s] = joined(rows[s][0], other)
        early = {0: first}
        lead = near[0] if near else None
        lead_stats = [block_stats(values[lead], rows[lead][1], w, c) for w, c in held] if near else []
        lead_stats, w_d, others = lax.optimization_barrier(
            (lead_stats, swap(w_p, "dl"), [swap(rows[s][0], "t") for s in far]))
        if near:
            early[lead] = lead_stats
        for s, other in zip(far, others):
            values[s] = joined(rows[s][0], other)
        for s in near[1:]:
            early[s] = [block_stats(values[s], rows[s][1], w, c) for w, c in held]
        pieces = held + ((w_d, cols[3]),)
        for s in range(n):
            if s in early:
                parts = early[s] + [block_stats(values[s], rows[s][1], w_d, cols[3])]
            else:
                parts = [block_stats(values[s], rows[s][1], w, c) for w, c in pieces]
            stats.append(combine(parts))
    else:
        w_pair = jnp.concatenate([head_weight, w_p], 1)
        w_all = jnp.concatenate([w_pair, swap(w_pair, "dl")], 1)
        for s in range(n):
            if n > 4:
                src = (dh - s) % n
                h_s, t_s = gathered_h[src], gathered_t[src]
                values = whole_rows(h_s, t, nt)
            elif s == 0:
                h_s, t_s = hidden_states, target_ids
                values = whole_rows(h_s, t, nt)
            else:
                h_s, t_s = moved[s - 1], moved_t[s - 1]
                values = whole_rows(h_s, t, nt)
            stats.append(block_stats(values, t_s, w_all))
    stats = jnp.stack(stats)
    stats = jnp.take(stats, (dh - jnp.arange(n)) % n, axis=0)
    rq = rb // nt
    stats = stats.reshape(n, 4, nt, rq).transpose(0, 2, 1, 3).reshape(n * nt, 4, rq)
    got = lax.all_to_all(stats, ("dh", "t"), 0, 0, tiled=True)
    tops, totals, spreads, pickeds = got[:, 0], got[:, 1], got[:, 2], got[:, 3]
    row_top = jnp.max(tops, axis=0)
    scale = jnp.exp(tops - row_top[None, :])
    row_total = jnp.sum(totals * scale, axis=0)
    row_spread = jnp.sum(scale * (spreads + totals * (tops - row_top[None, :])), axis=0)
    row_picked = jnp.sum(pickeds, axis=0)

    logsum = jnp.log(row_total)
    live = lax.dynamic_slice_in_dim(loss_mask, t * rq, rq).astype(jnp.float32)
    token_logprob = (row_picked - row_top - logsum) * live
    token_entropy = (logsum - row_spread / row_total) * live

    seqs = slot_order.shape[0]
    ends = jnp.cumsum(seq_lengths)
    position = b * rb + t * rq + jnp.arange(rq, dtype=jnp.int32)
    segment = jnp.sum((position[:, None] >= ends[None, :]).astype(jnp.int32), axis=1)
    member = (segment[:, None] == slot_order[None, :]).astype(jnp.float32)
    lp_part = jnp.dot(token_logprob, member, precision=lax.Precision.HIGHEST)
    ent_part = jnp.dot(token_entropy, member, precision=lax.Precision.HIGHEST)
    count_part = jnp.dot(live, member, precision=lax.Precision.HIGHEST)
    k = seqs // nd
    parts = jnp.stack([lp_part, ent_part, count_part]).reshape(3, nd, k).transpose(1, 0, 2)
    parts = jnp.broadcast_to(parts[:, None], (nd, nt, 3, k)).reshape(nd * nt, 3, k)
    sums = jnp.sum(lax.all_to_all(parts, ALL, 0, 0, tiled=True), axis=0)
    floor = jnp.maximum(sums[2], 1.0)
    return (token_logprob, token_entropy, sums[0] / floor, sums[1] / floor)


def solution(mesh):
    nd, nt = mesh.devices.shape
    grid = Mesh(mesh.devices.reshape(nd // 4, 2, 2, nt), ALL)
    placed = (P(ROWS, "t"), P(), P(None, ("t",) + ROWS), P(ROWS), P(ROWS), P(), P())
    return jax.shard_map(
        per_device,
        mesh=grid,
        in_specs=placed,
        out_specs=(P(ALL), P(ALL), P(ROWS), P(ROWS)),
        check_vma=False,
    )
```

profile of v0, /device:TPU:0, one launch (start us, length us, event | category | flops | bytes accessed | tf_op | source)
XLA Modules:
  0.0 181.9 jit_solution(2731043045141974428)
XLA Ops:
  1.1 2.6 %collective-permute-start = (bf16[512,1024]{1,0:T(8,128)(2,1)}, bf16[512,1024]{1,0:T(8,128)(2,1)}, u32[]{:S(2)}, u32[]{:S(2)}) collective-permute-start(bf16[512,1024]{1,0:T(8,128)(2,1)} %param.7), channel_id=1, source_target_pairs={{0,1},{1,0},{2,3},{3,2},{4,5},{5,4},{6,7},{7,6},{8,9},{9,8},{10,11... | collective-permute-start | bytes 3145736 | tf_op jit(solution)/shard_map/ppermute | solution.py:14
  3.7 0.7 fusion.71
  4.4 2.3 %maximum_maximum_fusion = bf16[513,1024]{1,0:T(8,128)(2,1)} fusion(bf16[1,512]{1,0:T(2,128)(2,1)S(1)} %concatenate.56, bf16[1,512]{1,0:T(2,128)(2,1)S(1)} %concatenate.55, bf16[512,1024]{1,0:T(8,128)(2,1)} %param.7), kind=kLoop, calls=%fused_computation.73 | loop fusion | flops 3151872 | bytes 2101248 | tf_op jit(solution)/shard_map/concatenate | solution.py:94
  6.7 1.6 collective-permute-start.2
  8.3 2.2 %collective-permute-start.3 = (bf16[513,1024]{1,0:T(8,128)(2,1)}, bf16[513,1024]{1,0:T(8,128)(2,1)}, u32[]{:S(2)}, u32[]{:S(2)}) collective-permute-start(bf16[513,1024]{1,0:T(8,128)(2,1)} %maximum_maximum_fusion), channel_id=1, source_target_pairs={{0,24},{8,0},{16,8},{24,16},{1,25},{9,1},{17,9},{25,17},{2,26},{10... | collective-permute-start | bytes 3151880 | tf_op jit(solution)/shard_map/ppermute | solution.py:29
  10.5 1.5 collective-permute-start.4
  12.1 0.7 convert_element_type.71
  12.7 0.7 copy.74
  14.0 2.3 %constant_dynamic-update-slice_fusion.1 = bf16[2048,1600]{0,1:T(8,128)(2,1)S(1)} fusion(bf16[2048,800]{0,1:T(8,128)(2,1)} %param.9), kind=kLoop, calls=%fused_computation.166 | loop fusion | bytes 6553600
  16.3 11.5 %collective-permute-done = bf16[512,1024]{1,0:T(8,128)(2,1)} collective-permute-done((bf16[512,1024]{1,0:T(8,128)(2,1)}, bf16[512,1024]{1,0:T(8,128)(2,1)}, u32[]{:S(2)}, u32[]{:S(2)}) %collective-permute-start) | collective-permute-done | bytes 1048608 | tf_op jit(solution)/shard_map/ppermute | solution.py:14
  27.8 2.9 %collective-permute-start.5 = (bf16[513,1024]{1,0:T(8,128)(2,1)}, bf16[513,1024]{1,0:T(8,128)(2,1)S(1)}, u32[]{:S(2)}, u32[]{:S(2)}) collective-permute-start(bf16[513,1024]{1,0:T(8,128)(2,1)} %maximum_maximum_fusion), channel_id=1, source_target_pairs={{0,16},{8,24},{16,0},{24,8},{1,17},{9,25},{17,1},{25,9},{2,18},{10... | collective-permute-start | bytes 3151880 | tf_op jit(solution)/shard_map/ppermute | solution.py:29
  30.6 4.6 %collective-permute-done.2 = bf16[513,1024]{1,0:T(8,128)(2,1)} collective-permute-done((bf16[513,1024]{1,0:T(8,128)(2,1)}, bf16[513,1024]{1,0:T(8,128)(2,1)}, u32[]{:S(2)}, u32[]{:S(2)}) %collective-permute-start.2) | collective-permute-done | bytes 1050656 | tf_op jit(solution)/shard_map/ppermute | solution.py:29
  35.2 21.5 %collective-permute-done.3 = bf16[513,1024]{1,0:T(8,128)(2,1)} collective-permute-done((bf16[513,1024]{1,0:T(8,128)(2,1)}, bf16[513,1024]{1,0:T(8,128)(2,1)}, u32[]{:S(2)}, u32[]{:S(2)}) %collective-permute-start.3) | collective-permute-done | bytes 1050656 | tf_op jit(solution)/shard_map/ppermute | solution.py:29
  56.7 1.3 slice.145
  58.0 0.6 collective-permute-start.6
  58.6 1.3 slice.146
  59.9 1.6 collective-permute-start.7
  61.5 2.3 %fusion = f32[512]{0:T(512)S(1)} fusion(bf16[512,1024]{1,0:T(8,128)(2,1)S(1)} %copy-done, bf16[512,1024]{1,0:T(8,128)(2,1)} %collective-permute-done, pred[]{:T(512)S(6)} %eq.61), kind=kLoop, calls=%fused_computation.17 | loop fusion | flops 12582400 | bytes 2099201 | tf_op jit(solution)/shard_map/reduce_sum | solution.py:64
  64.0 5.4 %fusion.108 = (f32[512]{0:T(512)S(1)}, f32[512,1600]{0,1:T(8,128)S(1)}) fusion(bf16[2048,1600]{0,1:T(8,128)(2,1)S(1)} %constant_dynamic-update-slice_fusion, f32[2048]{0:T(1024)S(1)} %convert_element_type.71, f32[512]{0:T(512)S(1)} %add_rsqrt_fusion.3, bf16[512,1024]{1,0:T(8,128)(2,1)S(1)} %copy-done, bf16[512,1024]{1,0:T(8,128)(2,1)} %collective-permute-done, ...), kind=kOutput, calls=%fused_computation.236 | convolution fusion | flops 3369893376 | bytes 11939841 | tf_op jit(solution)/shard_map/dot_general | solution.py:69
  69.5 1.6 exponential_reduce_fusion.3
  71.1 12.3 %collective-permute-done.4 = bf16[2048,800]{0,1:T(8,128)(2,1)} collective-permute-done((bf16[2048,800]{0,1:T(8,128)(2,1)}, bf16[2048,800]{0,1:T(8,128)(2,1)}, u32[]{:S(2)}, u32[]{:S(2)}) %collective-permute-start.4) | collective-permute-done | bytes 3276832 | tf_op jit(solution)/shard_map/ppermute | solution.py:14
  83.3 5.0 %fusion.109 = (f32[512]{0:T(512)S(1)}, f32[512,800]{0,1:T(8,128)S(1)}) fusion(bf16[2048,800]{0,1:T(8,128)(2,1)} %collective-permute-done.4, f32[2048]{0:T(1024)S(1)} %convert_element_type.71, f32[512]{0:T(512)S(1)} %add_rsqrt_fusion.3, bf16[512,1024]{1,0:T(8,128)(2,1)S(1)} %copy-done, bf16[512,1024]{1,0:T(8,128)(2,1)} %collective-permute-done, pred[]{:T(512)S(6)} %eq.61), kind=kOutput, calls=%fused_computation.237 | convolution fusion | flops 1691762176 | bytes 7024641 | tf_op jit(solution)/shard_map/dot_general | solution.py:69
  88.9 0.7 slice_convert_fusion.2
  89.7 0.7 slice_convert_fusion
  90.4 12.4 %collective-permute-done.5 = bf16[513,1024]{1,0:T(8,128)(2,1)S(1)} collective-permute-done((bf16[513,1024]{1,0:T(8,128)(2,1)}, bf16[513,1024]{1,0:T(8,128)(2,1)S(1)}, u32[]{:S(2)}, u32[]{:S(2)}) %collective-permute-start.5) | collective-permute-done | bytes 1050656 | tf_op jit(solution)/shard_map/ppermute | solution.py:29
  102.8 2.2 %collective-permute-done.7 = bf16[512,1024]{1,0:T(8,128)(2,1)S(1)} collective-permute-done((bf16[512,1024]{1,0:T(8,128)(2,1)S(1)}, bf16[512,1024]{1,0:T(8,128)(2,1)S(1)}, u32[]{:S(2)}, u32[]{:S(2)}) %collective-permute-start.7) | collective-permute-done | bytes 1048608 | tf_op jit(solution)/shard_map/ppermute | solution.py:14
  105.2 0.6 fusion.3
  106.4 0.6 fusion.9
  107.0 4.0 %fusion.111 = (f32[512]{0:T(512)S(1)}, f32[512,800]{0,1:T(8,128)S(1)}) fusion(bf16[2048,800]{0,1:T(8,128)(2,1)} %collective-permute-done.4, f32[512]{0:T(512)S(1)} %add_rsqrt_fusion.2, f32[2048]{0:T(1024)S(1)} %convert_element_type.71, bf16[512,1024]{1,0:T(8,128)(2,1)S(1)} %slice.145, bf16[512,1024]{1,0:T(8,128)(2,1)S(1)} %collective-permute-done.6, ...), kind=kOutput, calls=%fused_computation.239 | convolution fusion | flops 1691762176 | bytes 7024641 | tf_op jit(solution)/shard_map/dot_general | solution.py:69
  111.5 3.8 %fusion.110 = (f32[512]{0:T(512)S(1)}, f32[512,1600]{0,1:T(8,128)S(1)}) fusion(bf16[2048,1600]{0,1:T(8,128)(2,1)S(1)} %constant_dynamic-update-slice_fusion, f32[512]{0:T(512)S(1)} %add_rsqrt_fusion.2, f32[2048]{0:T(1024)S(1)} %convert_element_type.71, bf16[512,1024]{1,0:T(8,128)(2,1)S(1)} %slice.145, bf16[512,1024]{1,0:T(8,128)(2,1)S(1)} %collective-permute-done.6, ...), kind=kOutput, calls=%fused_computation.238 | convolution fusion | flops 3369893376 | bytes 11939841 | tf_op jit(solution)/shard_map/dot_general | solution.py:69
  115.4 1.6 exponential_reduce_fusion.2
  117.0 4.0 %fusion.116 = (f32[512]{0:T(512)S(1)}, f32[512,800]{0,1:T(8,128)S(1)}) fusion(bf16[2048,800]{0,1:T(8,128)(2,1)} %collective-permute-done.4, f32[512]{0:T(512)S(1)} %add_rsqrt_fusion, f32[2048]{0:T(1024)S(1)} %convert_element_type.71, bf16[512,1024]{1,0:T(8,128)(2,1)S(1)} %slice.146, bf16[512,1024]{1,0:T(8,128)(2,1)S(1)} %collective-permute-done.7, pred[]{:T(512)S(6)} %eq.61), kind=kOutput, calls=%fused_computation.244 | convolution fusion | flops 1691762176 | bytes 7024641 | tf_op jit(solution)/shard_map/dot_general | solution.py:69
  121.1 3.8 %fusion.119 = (f32[512]{0:T(512)S(1)}, f32[512,1600]{0,1:T(8,128)S(1)}) fusion(bf16[2048,1600]{0,1:T(8,128)(2,1)S(1)} %constant_dynamic-update-slice_fusion, f32[512]{0:T(512)S(1)} %add_rsqrt_fusion, f32[2048]{0:T(1024)S(1)} %convert_element_type.71, bf16[512,1024]{1,0:T(8,128)(2,1)S(1)} %slice.146, bf16[512,1024]{1,0:T(8,128)(2,1)S(1)} %collective-permute-done.7, ...), kind=kOutput, calls=%fused_computation.247 | convolution fusion | flops 3369893376 | bytes 11939841 | tf_op jit(solution)/shard_map/dot_general | solution.py:69
  124.9 4.6 %collective-permute-done.9 = bf16[512,1024]{1,0:T(8,128)(2,1)S(1)} collective-permute-done((bf16[512,1024]{1,0:T(8,128)(2,1)S(1)}, bf16[512,1024]{1,0:T(8,128)(2,1)S(1)}, u32[]{:S(2)}, u32[]{:S(2)}) %collective-permute-start.9) | collective-permute-done | bytes 1048608 | tf_op jit(solution)/shard_map/ppermute | solution.py:14
  129.4 4.3 %fusion.112 = (f32[512]{0:T(512)S(1)}, f32[512,800]{0,1:T(8,128)S(1)}) fusion(bf16[2048,800]{0,1:T(8,128)(2,1)S(1)} %collective-permute-done.8, f32[2048]{0:T(1024)S(1)} %convert_element_type.71, f32[512]{0:T(512)S(1)} %add_rsqrt_fusion.3, bf16[512,1024]{1,0:T(8,128)(2,1)S(1)} %copy-done, bf16[512,1024]{1,0:T(8,128)(2,1)} %collective-permute-done, pred[]{:T(512)S(6)} %eq.61), kind=kOutput, calls=%fused_computation.240 | convolution fusion | flops 1691762176 | bytes 7024641 | tf_op jit(solution)/shard_map/dot_general | solution.py:69
  133.7 2.0 %fusion.113 = (f32[512]{0:T(512)S(1)}, f32[512,800]{0,1:T(8,128)S(1)}) fusion(bf16[2048,800]{0,1:T(8,128)(2,1)S(1)} %collective-permute-done.8, f32[512]{0:T(512)S(1)} %add_rsqrt_fusion.2, f32[2048]{0:T(1024)S(1)} %convert_element_type.71, bf16[512,1024]{1,0:T(8,128)(2,1)S(1)} %slice.145, bf16[512,1024]{1,0:T(8,128)(2,1)S(1)} %collective-permute-done.6, ...), kind=kOutput, calls=%fused_computation.241 | convolution fusion | flops 1691762176 | bytes 7024641 | tf_op jit(solution)/shard_map/dot_general | solution.py:69
  135.8 2.1 %fusion.115 = (f32[512]{0:T(512)S(1)}, f32[512,800]{0,1:T(8,128)S(1)}) fusion(bf16[2048,800]{0,1:T(8,128)(2,1)S(1)} %collective-permute-done.8, f32[512]{0:T(512)S(1)} %add_rsqrt_fusion, f32[2048]{0:T(1024)S(1)} %convert_element_type.71, bf16[512,1024]{1,0:T(8,128)(2,1)S(1)} %slice.146, bf16[512,1024]{1,0:T(8,128)(2,1)S(1)} %collective-permute-done.7, ...), kind=kOutput, calls=%fused_computation.243 | convolution fusion | flops 1691762176 | bytes 7024641 | tf_op jit(solution)/shard_map/dot_general | solution.py:69
  137.8 0.6 fusion.6
  138.4 2.1 %fusion.114 = (f32[512]{0:T(512)S(1)}, f32[512,800]{0,1:T(8,128)S(1)}) fusion(bf16[2048,800]{0,1:T(8,128)(2,1)S(1)} %collective-permute-done.8, f32[512]{0:T(512)S(1)} %add_rsqrt_fusion.1, f32[2048]{0:T(1024)S(1)} %convert_element_type.71, bf16[512,1024]{1,0:T(8,128)(2,1)S(1)} %slice.150, bf16[512,1024]{1,0:T(8,128)(2,1)S(1)} %collective-permute-done.9, ...), kind=kOutput, calls=%fused_computation.242 | convolution fusion | flops 1691762176 | bytes 7024641 | tf_op jit(solution)/shard_map/dot_general | solution.py:69
  140.5 3.8 %fusion.118 = (f32[512]{0:T(512)S(1)}, f32[512,1600]{0,1:T(8,128)S(1)}) fusion(bf16[2048,1600]{0,1:T(8,128)(2,1)S(1)} %constant_dynamic-update-slice_fusion, f32[512]{0:T(512)S(1)} %add_rsqrt_fusion.1, f32[2048]{0:T(1024)S(1)} %convert_element_type.71, bf16[512,1024]{1,0:T(8,128)(2,1)S(1)} %slice.150, bf16[512,1024]{1,0:T(8,128)(2,1)S(1)} %collective-permute-done.9, ...), kind=kOutput, calls=%fused_computation.246 | convolution fusion | flops 3369893376 | bytes 11939841 | tf_op jit(solution)/shard_map/dot_general | solution.py:69
  144.3 4.0 %fusion.117 = (f32[512]{0:T(512)S(1)}, f32[512,800]{0,1:T(8,128)S(1)}) fusion(bf16[2048,800]{0,1:T(8,128)(2,1)} %collective-permute-done.4, f32[512]{0:T(512)S(1)} %add_rsqrt_fusion.1, f32[2048]{0:T(1024)S(1)} %convert_element_type.71, bf16[512,1024]{1,0:T(8,128)(2,1)S(1)} %slice.150, bf16[512,1024]{1,0:T(8,128)(2,1)S(1)} %collective-permute-done.9, ...), kind=kOutput, calls=%fused_computation.245 | convolution fusion | flops 1691762176 | bytes 7024641 | tf_op jit(solution)/shard_map/dot_general | solution.py:69
  148.3 3.6 %exponential_reduce_fusion.9 = (f32[512]{0:T(512)S(1)}, f32[512]{0:T(512)S(1)}, f32[512]{0:T(512)S(1)}, f32[512]{0:T(512)S(1)}, f32[512]{0:T(512)S(1)}, /*index=...) fusion(f32[512,800]{0,1:T(8,128)S(1)} %get-tuple-element.152, ...), kind=kLoop, calls=%fused_computation.48 | loop fusion | flops 17193984 | bytes 9894144 | tf_op jit(solution)/shard_map/reduce_sum | solution.py:73
  152.0 2.6 %exponential_reduce_fusion.1 = (f32[512]{0:T(512)S(1)}, f32[512]{0:T(512)S(1)}, f32[512]{0:T(512)S(1)}, f32[512]{0:T(512)S(1)}, f32[512]{0:T(512)S(1)}, /*index=5*/f32[512]{0:T(512)S(1)}) fusion(f32[512,1600]{0,1:T(8,128)S(1)} %get-tuple-element.164, f32[512]{0:T(512)S(1)} %get-tuple-element.163, s32[512]{0:T(512)S(1)} %bitcast.273, ...), kind=kLoop, calls=%fused_computation.12 | loop fusion | flops 11465728 | bytes 6580480 | tf_op jit(solution)/shard_map/reduce_sum | solution.py:73
  155.9 0.6 reshape.293
  156.5 3.6 %all-to-all-start = ((f32[8,4,256]{2,1,0:T(4,128)}), f32[8,4,256]{2,1,0:T(4,128)S(1)}, u32[]{:S(2)}, u32[]{:S(2)}) async-start(f32[8,4,256]{2,1,0:T(4,128)} %reshape.293), calls=%async_computation | async-start | bytes 65536 | tf_op jit(solution)/shard_map/all_to_all | solution.py:156
  160.3 6.6 %all-to-all-done = f32[8,4,256]{2,1,0:T(4,128)S(1)} async-done(((f32[8,4,256]{2,1,0:T(4,128)}), f32[8,4,256]{2,1,0:T(4,128)S(1)}, u32[]{:S(2)}, u32[]{:S(2)}) %all-to-all-start) | async-done | bytes 32800 | tf_op jit(solution)/shard_map/all_to_all | solution.py:156
  167.9 9.0 %all_to_all.10 = f32[32,3,1]{1,2,0:T(1,128)S(1)} all-to-all(f32[32,3,1]{1,2,0:T(1,128)S(1)} %bitcast.262), channel_id=1, replica_groups=mesh['dh'=4,'p'=2,'dl'=2,'t'=2] {'dh','p','dl','t'}, dimensions={0} | all-to-all | bytes 768 | tf_op jit(solution)/shard_map/all_to_all | solution.py:180
  176.9 0.7 fusion.107
  (85 shorter events, 5.4 us)
Async XLA Ops:
  0.6 56.1 %collective-permute-start.1 = (bf16[2048,800]{0,1:T(8,128)(2,1)}, bf16[2048,800]{0,1:T(8,128)(2,1)S(1)}, u32[]{:S(2)}, u32[]{:S(2)}) collective-permute-start(bf16[2048,800]{0,1:T(8,128)(2,1)} %param.9), channel_id=1, source_target_pairs={{0,2},{2,0},{1,3},{3,1},{4,6},{6,4},{5,7},{7,5},{8,10},{10,8},{9,1... | collective-permute-start | bytes 9830408 | tf_op jit(solution)/shard_map/ppermute | solution.py:14
  1.1 26.6 %collective-permute-start = (bf16[512,1024]{1,0:T(8,128)(2,1)}, bf16[512,1024]{1,0:T(8,128)(2,1)}, u32[]{:S(2)}, u32[]{:S(2)}) collective-permute-start(bf16[512,1024]{1,0:T(8,128)(2,1)} %param.7), channel_id=1, source_target_pairs={{0,1},{1,0},{2,3},{3,2},{4,5},{5,4},{6,7},{7,6},{8,9},{9,8},{10,11... | collective-permute-start | bytes 3145736 | tf_op jit(solution)/shard_map/ppermute | solution.py:14
  6.7 28.5 %collective-permute-start.2 = (bf16[513,1024]{1,0:T(8,128)(2,1)}, bf16[513,1024]{1,0:T(8,128)(2,1)}, u32[]{:S(2)}, u32[]{:S(2)}) collective-permute-start(bf16[513,1024]{1,0:T(8,128)(2,1)} %maximum_maximum_fusion), channel_id=1, source_target_pairs={{0,8},{8,16},{16,24},{24,0},{1,9},{9,17},{17,25},{25,1},{2,10},{10... | collective-permute-start | bytes 3151880 | tf_op jit(solution)/shard_map/ppermute | solution.py:29
  8.3 48.4 %collective-permute-start.3 = (bf16[513,1024]{1,0:T(8,128)(2,1)}, bf16[513,1024]{1,0:T(8,128)(2,1)}, u32[]{:S(2)}, u32[]{:S(2)}) collective-permute-start(bf16[513,1024]{1,0:T(8,128)(2,1)} %maximum_maximum_fusion), channel_id=1, source_target_pairs={{0,24},{8,0},{16,8},{24,16},{1,25},{9,1},{17,9},{25,17},{2,26},{10... | collective-permute-start | bytes 3151880 | tf_op jit(solution)/shard_map/ppermute | solution.py:29
  10.5 72.8 %collective-permute-start.4 = (bf16[2048,800]{0,1:T(8,128)(2,1)}, bf16[2048,800]{0,1:T(8,128)(2,1)}, u32[]{:S(2)}, u32[]{:S(2)}) collective-permute-start(bf16[2048,800]{0,1:T(8,128)(2,1)} %param.9), channel_id=1, source_target_pairs={{0,4},{4,0},{1,5},{5,1},{2,6},{6,2},{3,7},{7,3},{8,12},{12,8},{9,1... | collective-permute-start | bytes 9830408 | tf_op jit(solution)/shard_map/ppermute | solution.py:14
  16.3 45.2 %copy-start = (bf16[512,1024]{1,0:T(8,128)(2,1)S(1)}, bf16[512,1024]{1,0:T(8,128)(2,1)}, u32[]{:S(2)}) copy-start(bf16[512,1024]{1,0:T(8,128)(2,1)} %param.7) | copy-start | bytes 3145732
  27.8 75.0 %collective-permute-start.5 = (bf16[513,1024]{1,0:T(8,128)(2,1)}, bf16[513,1024]{1,0:T(8,128)(2,1)S(1)}, u32[]{:S(2)}, u32[]{:S(2)}) collective-permute-start(bf16[513,1024]{1,0:T(8,128)(2,1)} %maximum_maximum_fusion), channel_id=1, source_target_pairs={{0,16},{8,24},{16,0},{24,8},{1,17},{9,25},{17,1},{25,9},{2,18},{10... | collective-permute-start | bytes 3151880 | tf_op jit(solution)/shard_map/ppermute | solution.py:29
  58.0 44.8 %collective-permute-start.6 = (bf16[512,1024]{1,0:T(8,128)(2,1)S(1)}, bf16[512,1024]{1,0:T(8,128)(2,1)S(1)}, u32[]{:S(2)}, u32[]{:S(2)}) collective-permute-start(bf16[512,1024]{1,0:T(8,128)(2,1)S(1)} %slice.145), channel_id=1, source_target_pairs={{0,1},{1,0},{2,3},{3,2},{4,5},{5,4},{6,7},{7,6},{8,9},{9,8},{10,11... | collective-permute-start | bytes 3145736 | tf_op jit(solution)/shard_map/ppermute | solution.py:14
  59.9 45.1 %collective-permute-start.7 = (bf16[512,1024]{1,0:T(8,128)(2,1)S(1)}, bf16[512,1024]{1,0:T(8,128)(2,1)S(1)}, u32[]{:S(2)}, u32[]{:S(2)}) collective-permute-start(bf16[512,1024]{1,0:T(8,128)(2,1)S(1)} %slice.146), channel_id=1, source_target_pairs={{0,1},{1,0},{2,3},{3,2},{4,5},{5,4},{6,7},{7,6},{8,9},{9,8},{10,11... | collective-permute-start | bytes 3145736 | tf_op jit(solution)/shard_map/ppermute | solution.py:14
  64.0 5.4 %copy-start.1 = (s32[512]{0:T(512)S(1)}, s32[512]{0:T(512)}, u32[]{:S(2)}) copy-start(s32[512]{0:T(512)} %param.10) | copy-start | bytes 6148
  88.8 40.6 %collective-permute-start.8 = (bf16[2048,800]{0,1:T(8,128)(2,1)}, bf16[2048,800]{0,1:T(8,128)(2,1)S(1)}, u32[]{:S(2)}, u32[]{:S(2)}) collective-permute-start(bf16[2048,800]{0,1:T(8,128)(2,1)} %collective-permute-done.4), channel_id=1, source_target_pairs={{0,2},{2,0},{1,3},{3,1},{4,6},{6,4},{5,7},{7,5},{8,10},{10,8},{9,1... | collective-permute-start | bytes 9830408 | tf_op jit(solution)/shard_map/ppermute | solution.py:14
  105.8 23.6 %collective-permute-start.9 = (bf16[512,1024]{1,0:T(8,128)(2,1)S(1)}, bf16[512,1024]{1,0:T(8,128)(2,1)S(1)}, u32[]{:S(2)}, u32[]{:S(2)}) collective-permute-start(bf16[512,1024]{1,0:T(8,128)(2,1)S(1)} %slice.150), channel_id=1, source_target_pairs={{0,1},{1,0},{2,3},{3,2},{4,5},{5,4},{6,7},{7,6},{8,9},{9,8},{10,11... | collective-permute-start | bytes 3145736 | tf_op jit(solution)/shard_map/ppermute | solution.py:14
  152.0 14.9 %copy-start.4 = (s32[512]{0:T(512)S(1)}, s32[512]{0:T(512)}, u32[]{:S(2)}) copy-start(s32[512]{0:T(512)} %param.11) | copy-start | bytes 6148
  152.0 15.0 %copy-start.5 = (s32[16]{0:T(128)S(1)}, s32[16]{0:T(128)}, u32[]{:S(2)}) copy-start(s32[16]{0:T(128)} %param.13) | copy-start | bytes 196
  156.5 10.3 %all-to-all-start = ((f32[8,4,256]{2,1,0:T(4,128)}), f32[8,4,256]{2,1,0:T(4,128)S(1)}, u32[]{:S(2)}, u32[]{:S(2)}) async-start(f32[8,4,256]{2,1,0:T(4,128)} %reshape.293), calls=%async_computation | async-start | bytes 65536 | tf_op jit(solution)/shard_map/all_to_all | solution.py:156
  167.0 12.6 %copy-start.3 = (f32[256]{0:T(256)}, f32[256]{0:T(256)S(1)}, u32[]{:S(2)}) copy-start(f32[256]{0:T(256)S(1)} %get-tuple-element.90) | copy-start | bytes 3076
  167.0 12.6 %copy-start.2 = (f32[256]{0:T(256)}, f32[256]{0:T(256)S(1)}, u32[]{:S(2)}) copy-start(f32[256]{0:T(256)S(1)} %subtract_multiply_fusion.1) | copy-start | bytes 3076
where the time goes:
time: 183 us; the launch traced here: 182 us
  waiting for transfers between devices  75.7 us (41%)
  matrix products  44.9 us (25%)
  other arithmetic  21.2 us (12%)
  starting transfers between devices  17.7 us (10%)
  blocking collectives  9.01 us (5%)
  local copies, waits for them, and re-layouts  7.97 us (4%)
  between operations  5.33 us (3%)
    dot_general x12, matrix products, block_stats(): jnp.dot(normalize(values), w_all, preferred_element_type=jnp.float32)  44.2 us
    ppermute x3, waiting for transfers between devices, shifted(): return lax.ppermute(x, 'dh', [(i, (i + s) % n) for i in range(n)])  38.5 us
    ppermute x7, waiting for transfers between devices, swap(): return lax.ppermute(x, name, [(0, 1), (1, 0)])  30.6 us
    reduce_sum x6, other arithmetic, block_stats(): total = jnp.sum(expo, axis=1)  10.5 us
    all_to_all x1, blocking collectives, per_device(): sums = jnp.sum(lax.all_to_all(parts, ALL, 0, 0, tiled=True), axis=0)  9.01 us
    ppermute x7, starting transfers between devices, swap(): return lax.ppermute(x, name, [(0, 1), (1, 0)])  7.43 us
    ppermute x3, starting transfers between devices, shifted(): return lax.ppermute(x, 'dh', [(i, (i + s) % n) for i in range(n)])  6.68 us
    all_to_all x1, waiting for transfers between devices, per_device(): got = lax.all_to_all(stats, ('dh', 't'), 0, 0, tiled=True)  6.6 us
  transfers between devices with their start and end apart: 11, of which 8 were waited for; matrix products, arithmetic and copies ran while one was open for 25% of the time, Pallas kernels for 0%

commit v1 on v0

--- a/solution.py
+++ b/solution.py
@@ -170,12 +170,11 @@
     ends = jnp.cumsum(seq_lengths)
     position = b * rb + t * rq + jnp.arange(rq, dtype=jnp.int32)
     segment = jnp.sum((position[:, None] >= ends[None, :]).astype(jnp.int32), axis=1)
-    member = (segment[:, None] == slot_order[None, :]).astype(jnp.float32)
-    lp_part = jnp.dot(token_logprob, member, precision=lax.Precision.HIGHEST)
-    ent_part = jnp.dot(token_entropy, member, precision=lax.Precision.HIGHEST)
-    count_part = jnp.dot(live, member, precision=lax.Precision.HIGHEST)
+    member = segment[:, None] == slot_order[None, :]
+    rowwise = jnp.stack([token_logprob, token_entropy, live])
     k = seqs // nd
-    parts = jnp.stack([lp_part, ent_part, count_part]).reshape(3, nd, k).transpose(1, 0, 2)
+    parts = jnp.sum(jnp.where(member[None], rowwise[:, :, None], 0.0), axis=1)
+    parts = parts.reshape(3, nd, k).transpose(1, 0, 2)
     parts = jnp.broadcast_to(parts[:, None], (nd, nt, 3, k)).reshape(nd * nt, 3, k)
     sums = jnp.sum(lax.all_to_all(parts, ALL, 0, 0, tiled=True), axis=0)
     floor = jnp.maximum(sums[2], 1.0)

time: 183 us -> 182 us (level)
  no operation moved by 1% of the time
where the time goes in v1:
time: 182 us; the launch traced here: 181 us
  waiting for transfers between devices  75.6 us (42%)
  matrix products  44.2 us (24%)
  other arithmetic  21.3 us (12%)
  starting transfers between devices  17.7 us (10%)
  blocking collectives  9.01 us (5%)
  local copies, waits for them, and re-layouts  7.98 us (4%)
  between operations  5.33 us (3%)
    dot_general x12, matrix products, block_stats(): jnp.dot(normalize(values), w_all, preferred_element_type=jnp.float32)  44.2 us
    ppermute x3, waiting for transfers between devices, shifted(): return lax.ppermute(x, 'dh', [(i, (i + s) % n) for i in range(n)])  38.5 us
    ppermute x7, waiting for transfers between devices, swap(): return lax.ppermute(x, name, [(0, 1), (1, 0)])  30.5 us
    reduce_sum x6, other arithmetic, block_stats(): total = jnp.sum(expo, axis=1)  10.5 us
    all_to_all x1, blocking collectives, per_device(): sums = jnp.sum(lax.all_to_all(parts, ALL, 0, 0, tiled=True), axis=0)  9.01 us
    ppermute x7, starting transfers between devices, swap(): return lax.ppermute(x, name, [(0, 1), (1, 0)])  7.43 us
    ppermute x3, starting transfers between devices, shifted(): return lax.ppermute(x, 'dh', [(i, (i + s) % n) for i in range(n)])  6.68 us
    all_to_all x1, waiting for transfers between devices, per_device(): got = lax.all_to_all(stats, ('dh', 't'), 0, 0, tiled=True)  6.61 us
  transfers between devices with their start and end apart: 11, of which 8 were waited for; matrix products, arithmetic and copies ran while one was open for 25% of the time, Pallas kernels for 0%

profile of v1, /device:TPU:0, one launch (start us, length us, event | category | flops | bytes accessed | tf_op | source)
XLA Modules:
  0.0 181.3 jit_solution(8232843907036260872)
XLA Ops:
  1.1 2.6 %collective-permute-start = (bf16[512,1024]{1,0:T(8,128)(2,1)}, bf16[512,1024]{1,0:T(8,128)(2,1)}, u32[]{:S(2)}, u32[]{:S(2)}) collective-permute-start(bf16[512,1024]{1,0:T(8,128)(2,1)} %param.7), channel_id=1, source_target_pairs={{0,1},{1,0},{2,3},{3,2},{4,5},{5,4},{6,7},{7,6},{8,9},{9,8},{10,11... | collective-permute-start | bytes 3145736 | tf_op jit(solution)/shard_map/ppermute | solution.py:14
  3.7 0.7 fusion.59
  4.4 2.3 %maximum_maximum_fusion = bf16[513,1024]{1,0:T(8,128)(2,1)} fusion(bf16[1,512]{1,0:T(2,128)(2,1)S(1)} %concatenate.56, bf16[1,512]{1,0:T(2,128)(2,1)S(1)} %concatenate.55, bf16[512,1024]{1,0:T(8,128)(2,1)} %param.7), kind=kLoop, calls=%fused_computation.73 | loop fusion | flops 3151872 | bytes 2101248 | tf_op jit(solution)/shard_map/concatenate | solution.py:94
  6.7 1.6 collective-permute-start.2
  8.3 2.2 %collective-permute-start.3 = (bf16[513,1024]{1,0:T(8,128)(2,1)}, bf16[513,1024]{1,0:T(8,128)(2,1)}, u32[]{:S(2)}, u32[]{:S(2)}) collective-permute-start(bf16[513,1024]{1,0:T(8,128)(2,1)} %maximum_maximum_fusion), channel_id=1, source_target_pairs={{0,24},{8,0},{16,8},{24,16},{1,25},{9,1},{17,9},{25,17},{2,26},{10... | collective-permute-start | bytes 3151880 | tf_op jit(solution)/shard_map/ppermute | solution.py:29
  10.5 1.5 collective-permute-start.4
  12.1 0.7 convert_element_type.70
  12.7 0.7 copy.74
  14.1 2.3 %constant_dynamic-update-slice_fusion.1 = bf16[2048,1600]{0,1:T(8,128)(2,1)S(1)} fusion(bf16[2048,800]{0,1:T(8,128)(2,1)} %param.9), kind=kLoop, calls=%fused_computation.156 | loop fusion | bytes 6553600
  16.4 11.4 %collective-permute-done = bf16[512,1024]{1,0:T(8,128)(2,1)} collective-permute-done((bf16[512,1024]{1,0:T(8,128)(2,1)}, bf16[512,1024]{1,0:T(8,128)(2,1)}, u32[]{:S(2)}, u32[]{:S(2)}) %collective-permute-start) | collective-permute-done | bytes 1048608 | tf_op jit(solution)/shard_map/ppermute | solution.py:14
  27.8 2.9 %collective-permute-start.5 = (bf16[513,1024]{1,0:T(8,128)(2,1)}, bf16[513,1024]{1,0:T(8,128)(2,1)S(1)}, u32[]{:S(2)}, u32[]{:S(2)}) collective-permute-start(bf16[513,1024]{1,0:T(8,128)(2,1)} %maximum_maximum_fusion), channel_id=1, source_target_pairs={{0,16},{8,24},{16,0},{24,8},{1,17},{9,25},{17,1},{25,9},{2,18},{10... | collective-permute-start | bytes 3151880 | tf_op jit(solution)/shard_map/ppermute | solution.py:29
  30.6 4.6 %collective-permute-done.2 = bf16[513,1024]{1,0:T(8,128)(2,1)} collective-permute-done((bf16[513,1024]{1,0:T(8,128)(2,1)}, bf16[513,1024]{1,0:T(8,128)(2,1)}, u32[]{:S(2)}, u32[]{:S(2)}) %collective-permute-start.2) | collective-permute-done | bytes 1050656 | tf_op jit(solution)/shard_map/ppermute | solution.py:29
  35.2 21.5 %collective-permute-done.3 = bf16[513,1024]{1,0:T(8,128)(2,1)} collective-permute-done((bf16[513,1024]{1,0:T(8,128)(2,1)}, bf16[513,1024]{1,0:T(8,128)(2,1)}, u32[]{:S(2)}, u32[]{:S(2)}) %collective-permute-start.3) | collective-permute-done | bytes 1050656 | tf_op jit(solution)/shard_map/ppermute | solution.py:29
  56.7 1.3 slice.145
  58.0 0.6 collective-permute-start.6
  58.6 1.3 slice.146
  59.9 1.6 collective-permute-start.7
  61.5 2.3 %fusion = f32[512]{0:T(512)S(1)} fusion(bf16[512,1024]{1,0:T(8,128)(2,1)S(1)} %copy-done, bf16[512,1024]{1,0:T(8,128)(2,1)} %collective-permute-done, pred[]{:T(512)S(6)} %eq.65), kind=kLoop, calls=%fused_computation.17 | loop fusion | flops 12582400 | bytes 2099201 | tf_op jit(solution)/shard_map/reduce_sum | solution.py:64
  64.0 5.4 %fusion.96 = (f32[512]{0:T(512)S(1)}, f32[512,1600]{0,1:T(8,128)S(1)}) fusion(bf16[2048,1600]{0,1:T(8,128)(2,1)S(1)} %constant_dynamic-update-slice_fusion, f32[2048]{0:T(1024)S(1)} %convert_element_type.70, f32[512]{0:T(512)S(1)} %add_rsqrt_fusion.3, bf16[512,1024]{1,0:T(8,128)(2,1)S(1)} %copy-done, bf16[512,1024]{1,0:T(8,128)(2,1)} %collective-permute-done, ...), kind=kOutput, calls=%fused_computation.226 | convolution fusion | flops 3369893376 | bytes 11939841 | tf_op jit(solution)/shard_map/dot_general | solution.py:69
  69.5 1.6 exponential_reduce_fusion.3
  71.1 12.3 %collective-permute-done.4 = bf16[2048,800]{0,1:T(8,128)(2,1)} collective-permute-done((bf16[2048,800]{0,1:T(8,128)(2,1)}, bf16[2048,800]{0,1:T(8,128)(2,1)}, u32[]{:S(2)}, u32[]{:S(2)}) %collective-permute-start.4) | collective-permute-done | bytes 3276832 | tf_op jit(solution)/shard_map/ppermute | solution.py:14
  83.3 5.0 %fusion.97 = (f32[512]{0:T(512)S(1)}, f32[512,800]{0,1:T(8,128)S(1)}) fusion(bf16[2048,800]{0,1:T(8,128)(2,1)} %collective-permute-done.4, f32[2048]{0:T(1024)S(1)} %convert_element_type.70, f32[512]{0:T(512)S(1)} %add_rsqrt_fusion.3, bf16[512,1024]{1,0:T(8,128)(2,1)S(1)} %copy-done, bf16[512,1024]{1,0:T(8,128)(2,1)} %collective-permute-done, pred[]{:T(512)S(6)} %eq.65), kind=kOutput, calls=%fused_computation.227 | convolution fusion | flops 1691762176 | bytes 7024641 | tf_op jit(solution)/shard_map/dot_general | solution.py:69
  88.9 0.7 slice_convert_fusion.2
  89.7 0.7 slice_convert_fusion
  90.4 12.4 %collective-permute-done.5 = bf16[513,1024]{1,0:T(8,128)(2,1)S(1)} collective-permute-done((bf16[513,1024]{1,0:T(8,128)(2,1)}, bf16[513,1024]{1,0:T(8,128)(2,1)S(1)}, u32[]{:S(2)}, u32[]{:S(2)}) %collective-permute-start.5) | collective-permute-done | bytes 1050656 | tf_op jit(solution)/shard_map/ppermute | solution.py:29
  102.8 2.2 %collective-permute-done.7 = bf16[512,1024]{1,0:T(8,128)(2,1)S(1)} collective-permute-done((bf16[512,1024]{1,0:T(8,128)(2,1)S(1)}, bf16[512,1024]{1,0:T(8,128)(2,1)S(1)}, u32[]{:S(2)}, u32[]{:S(2)}) %collective-permute-start.7) | collective-permute-done | bytes 1048608 | tf_op jit(solution)/shard_map/ppermute | solution.py:14
  105.2 0.6 fusion.3
  106.4 0.6 fusion.9
  107.0 4.0 %fusion.99 = (f32[512]{0:T(512)S(1)}, f32[512,800]{0,1:T(8,128)S(1)}) fusion(bf16[2048,800]{0,1:T(8,128)(2,1)} %collective-permute-done.4, f32[512]{0:T(512)S(1)} %add_rsqrt_fusion.2, f32[2048]{0:T(1024)S(1)} %convert_element_type.70, bf16[512,1024]{1,0:T(8,128)(2,1)S(1)} %slice.145, bf16[512,1024]{1,0:T(8,128)(2,1)S(1)} %collective-permute-done.6, ...), kind=kOutput, calls=%fused_computation.229 | convolution fusion | flops 1691762176 | bytes 7024641 | tf_op jit(solution)/shard_map/dot_general | solution.py:69
  111.5 3.8 %fusion.98 = (f32[512]{0:T(512)S(1)}, f32[512,1600]{0,1:T(8,128)S(1)}) fusion(bf16[2048,1600]{0,1:T(8,128)(2,1)S(1)} %constant_dynamic-update-slice_fusion, f32[512]{0:T(512)S(1)} %add_rsqrt_fusion.2, f32[2048]{0:T(1024)S(1)} %convert_element_type.70, bf16[512,1024]{1,0:T(8,128)(2,1)S(1)} %slice.145, bf16[512,1024]{1,0:T(8,128)(2,1)S(1)} %collective-permute-done.6, ...), kind=kOutput, calls=%fused_computation.228 | convolution fusion | flops 3369893376 | bytes 11939841 | tf_op jit(solution)/shard_map/dot_general | solution.py:69
  115.4 1.6 exponential_reduce_fusion.2
  117.0 4.0 %fusion.104 = (f32[512]{0:T(512)S(1)}, f32[512,800]{0,1:T(8,128)S(1)}) fusion(bf16[2048,800]{0,1:T(8,128)(2,1)} %collective-permute-done.4, f32[512]{0:T(512)S(1)} %add_rsqrt_fusion, f32[2048]{0:T(1024)S(1)} %convert_element_type.70, bf16[512,1024]{1,0:T(8,128)(2,1)S(1)} %slice.146, bf16[512,1024]{1,0:T(8,128)(2,1)S(1)} %collective-permute-done.7, pred[]{:T(512)S(6)} %eq.65), kind=kOutput, calls=%fused_computation.234 | convolution fusion | flops 1691762176 | bytes 7024641 | tf_op jit(solution)/shard_map/dot_general | solution.py:69
  121.1 3.8 %fusion.107 = (f32[512]{0:T(512)S(1)}, f32[512,1600]{0,1:T(8,128)S(1)}) fusion(bf16[2048,1600]{0,1:T(8,128)(2,1)S(1)} %constant_dynamic-update-slice_fusion, f32[512]{0:T(512)S(1)} %add_rsqrt_fusion, f32[2048]{0:T(1024)S(1)} %convert_element_type.70, bf16[512,1024]{1,0:T(8,128)(2,1)S(1)} %slice.146, bf16[512,1024]{1,0:T(8,128)(2,1)S(1)} %collective-permute-done.7, ...), kind=kOutput, calls=%fused_computation.237 | convolution fusion | flops 3369893376 | bytes 11939841 | tf_op jit(solution)/shard_map/dot_general | solution.py:69
  124.9 4.6 %collective-permute-done.9 = bf16[512,1024]{1,0:T(8,128)(2,1)S(1)} collective-permute-done((bf16[512,1024]{1,0:T(8,128)(2,1)S(1)}, bf16[512,1024]{1,0:T(8,128)(2,1)S(1)}, u32[]{:S(2)}, u32[]{:S(2)}) %collective-permute-start.9) | collective-permute-done | bytes 1048608 | tf_op jit(solution)/shard_map/ppermute | solution.py:14
  129.4 4.3 %fusion.100 = (f32[512]{0:T(512)S(1)}, f32[512,800]{0,1:T(8,128)S(1)}) fusion(bf16[2048,800]{0,1:T(8,128)(2,1)S(1)} %collective-permute-done.8, f32[2048]{0:T(1024)S(1)} %convert_element_type.70, f32[512]{0:T(512)S(1)} %add_rsqrt_fusion.3, bf16[512,1024]{1,0:T(8,128)(2,1)S(1)} %copy-done, bf16[512,1024]{1,0:T(8,128)(2,1)} %collective-permute-done, pred[]{:T(512)S(6)} %eq.65), kind=kOutput, calls=%fused_computation.230 | convolution fusion | flops 1691762176 | bytes 7024641 | tf_op jit(solution)/shard_map/dot_general | solution.py:69
  133.7 2.0 %fusion.101 = (f32[512]{0:T(512)S(1)}, f32[512,800]{0,1:T(8,128)S(1)}) fusion(bf16[2048,800]{0,1:T(8,128)(2,1)S(1)} %collective-permute-done.8, f32[512]{0:T(512)S(1)} %add_rsqrt_fusion.2, f32[2048]{0:T(1024)S(1)} %convert_element_type.70, bf16[512,1024]{1,0:T(8,128)(2,1)S(1)} %slice.145, bf16[512,1024]{1,0:T(8,128)(2,1)S(1)} %collective-permute-done.6, ...), kind=kOutput, calls=%fused_computation.231 | convolution fusion | flops 1691762176 | bytes 7024641 | tf_op jit(solution)/shard_map/dot_general | solution.py:69
  135.8 2.1 %fusion.103 = (f32[512]{0:T(512)S(1)}, f32[512,800]{0,1:T(8,128)S(1)}) fusion(bf16[2048,800]{0,1:T(8,128)(2,1)S(1)} %collective-permute-done.8, f32[512]{0:T(512)S(1)} %add_rsqrt_fusion, f32[2048]{0:T(1024)S(1)} %convert_element_type.70, bf16[512,1024]{1,0:T(8,128)(2,1)S(1)} %slice.146, bf16[512,1024]{1,0:T(8,128)(2,1)S(1)} %collective-permute-done.7, ...), kind=kOutput, calls=%fused_computation.233 | convolution fusion | flops 1691762176 | bytes 7024641 | tf_op jit(solution)/shard_map/dot_general | solution.py:69
  137.8 0.6 fusion.6
  138.4 2.1 %fusion.102 = (f32[512]{0:T(512)S(1)}, f32[512,800]{0,1:T(8,128)S(1)}) fusion(bf16[2048,800]{0,1:T(8,128)(2,1)S(1)} %collective-permute-done.8, f32[512]{0:T(512)S(1)} %add_rsqrt_fusion.1, f32[2048]{0:T(1024)S(1)} %convert_element_type.70, bf16[512,1024]{1,0:T(8,128)(2,1)S(1)} %slice.150, bf16[512,1024]{1,0:T(8,128)(2,1)S(1)} %collective-permute-done.9, ...), kind=kOutput, calls=%fused_computation.232 | convolution fusion | flops 1691762176 | bytes 7024641 | tf_op jit(solution)/shard_map/dot_general | solution.py:69
  140.5 3.8 %fusion.106 = (f32[512]{0:T(512)S(1)}, f32[512,1600]{0,1:T(8,128)S(1)}) fusion(bf16[2048,1600]{0,1:T(8,128)(2,1)S(1)} %constant_dynamic-update-slice_fusion, f32[512]{0:T(512)S(1)} %add_rsqrt_fusion.1, f32[2048]{0:T(1024)S(1)} %convert_element_type.70, bf16[512,1024]{1,0:T(8,128)(2,1)S(1)} %slice.150, bf16[512,1024]{1,0:T(8,128)(2,1)S(1)} %collective-permute-done.9, ...), kind=kOutput, calls=%fused_computation.236 | convolution fusion | flops 3369893376 | bytes 11939841 | tf_op jit(solution)/shard_map/dot_general | solution.py:69
  144.3 4.0 %fusion.105 = (f32[512]{0:T(512)S(1)}, f32[512,800]{0,1:T(8,128)S(1)}) fusion(bf16[2048,800]{0,1:T(8,128)(2,1)} %collective-permute-done.4, f32[512]{0:T(512)S(1)} %add_rsqrt_fusion.1, f32[2048]{0:T(1024)S(1)} %convert_element_type.70, bf16[512,1024]{1,0:T(8,128)(2,1)S(1)} %slice.150, bf16[512,1024]{1,0:T(8,128)(2,1)S(1)} %collective-permute-done.9, ...), kind=kOutput, calls=%fused_computation.235 | convolution fusion | flops 1691762176 | bytes 7024641 | tf_op jit(solution)/shard_map/dot_general | solution.py:69
  148.3 3.6 %exponential_reduce_fusion.9 = (f32[512]{0:T(512)S(1)}, f32[512]{0:T(512)S(1)}, f32[512]{0:T(512)S(1)}, f32[512]{0:T(512)S(1)}, f32[512]{0:T(512)S(1)}, /*index=...) fusion(f32[512,800]{0,1:T(8,128)S(1)} %get-tuple-element.152, ...), kind=kLoop, calls=%fused_computation.48 | loop fusion | flops 17193984 | bytes 9894144 | tf_op jit(solution)/shard_map/reduce_sum | solution.py:73
  152.0 2.6 %exponential_reduce_fusion.1 = (f32[512]{0:T(512)S(1)}, f32[512]{0:T(512)S(1)}, f32[512]{0:T(512)S(1)}, f32[512]{0:T(512)S(1)}, f32[512]{0:T(512)S(1)}, /*index=5*/f32[512]{0:T(512)S(1)}) fusion(f32[512,1600]{0,1:T(8,128)S(1)} %get-tuple-element.164, f32[512]{0:T(512)S(1)} %get-tuple-element.163, s32[512]{0:T(512)S(1)} %bitcast.266, ...), kind=kLoop, calls=%fused_computation.12 | loop fusion | flops 11465728 | bytes 6580480 | tf_op jit(solution)/shard_map/reduce_sum | solution.py:73
  155.9 0.6 reshape.319
  156.5 3.6 %all-to-all-start = ((f32[8,4,256]{2,1,0:T(4,128)}), f32[8,4,256]{2,1,0:T(4,128)S(1)}, u32[]{:S(2)}, u32[]{:S(2)}) async-start(f32[8,4,256]{2,1,0:T(4,128)} %reshape.319), calls=%async_computation | async-start | bytes 65536 | tf_op jit(solution)/shard_map/all_to_all | solution.py:156
  160.3 6.6 %all-to-all-done = f32[8,4,256]{2,1,0:T(4,128)S(1)} async-done(((f32[8,4,256]{2,1,0:T(4,128)}), f32[8,4,256]{2,1,0:T(4,128)S(1)}, u32[]{:S(2)}, u32[]{:S(2)}) %all-to-all-start) | async-done | bytes 32800 | tf_op jit(solution)/shard_map/all_to_all | solution.py:156
  167.2 9.0 %all_to_all.10 = f32[32,3,1]{1,2,0:T(1,128)S(1)} all-to-all(f32[32,3,1]{1,2,0:T(1,128)S(1)} %bitcast.255), channel_id=1, replica_groups=mesh['dh'=4,'p'=2,'dl'=2,'t'=2] {'dh','p','dl','t'}, dimensions={0} | all-to-all | bytes 768 | tf_op jit(solution)/shard_map/all_to_all | solution.py:179
  176.3 0.7 fusion.95
  (84 shorter events, 4.9 us)
Async XLA Ops:
  0.6 56.1 %collective-permute-start.1 = (bf16[2048,800]{0,1:T(8,128)(2,1)}, bf16[2048,800]{0,1:T(8,128)(2,1)S(1)}, u32[]{:S(2)}, u32[]{:S(2)}) collective-permute-start(bf16[2048,800]{0,1:T(8,128)(2,1)} %param.9), channel_id=1, source_target_pairs={{0,2},{2,0},{1,3},{3,1},{4,6},{6,4},{5,7},{7,5},{8,10},{10,8},{9,1... | collective-permute-start | bytes 9830408 | tf_op jit(solution)/shard_map/ppermute | solution.py:14
  1.1 26.6 %collective-permute-start = (bf16[512,1024]{1,0:T(8,128)(2,1)}, bf16[512,1024]{1,0:T(8,128)(2,1)}, u32[]{:S(2)}, u32[]{:S(2)}) collective-permute-start(bf16[512,1024]{1,0:T(8,128)(2,1)} %param.7), channel_id=1, source_target_pairs={{0,1},{1,0},{2,3},{3,2},{4,5},{5,4},{6,7},{7,6},{8,9},{9,8},{10,11... | collective-permute-start | bytes 3145736 | tf_op jit(solution)/shard_map/ppermute | solution.py:14
  6.7 28.5 %collective-permute-start.2 = (bf16[513,1024]{1,0:T(8,128)(2,1)}, bf16[513,1024]{1,0:T(8,128)(2,1)}, u32[]{:S(2)}, u32[]{:S(2)}) collective-permute-start(bf16[513,1024]{1,0:T(8,128)(2,1)} %maximum_maximum_fusion), channel_id=1, source_target_pairs={{0,8},{8,16},{16,24},{24,0},{1,9},{9,17},{17,25},{25,1},{2,10},{10... | collective-permute-start | bytes 3151880 | tf_op jit(solution)/shard_map/ppermute | solution.py:29
  8.3 48.4 %collective-permute-start.3 = (bf16[513,1024]{1,0:T(8,128)(2,1)}, bf16[513,1024]{1,0:T(8,128)(2,1)}, u32[]{:S(2)}, u32[]{:S(2)}) collective-permute-start(bf16[513,1024]{1,0:T(8,128)(2,1)} %maximum_maximum_fusion), channel_id=1, source_target_pairs={{0,24},{8,0},{16,8},{24,16},{1,25},{9,1},{17,9},{25,17},{2,26},{10... | collective-permute-start | bytes 3151880 | tf_op jit(solution)/shard_map/ppermute | solution.py:29
  10.5 72.8 %collective-permute-start.4 = (bf16[2048,800]{0,1:T(8,128)(2,1)}, bf16[2048,800]{0,1:T(8,128)(2,1)}, u32[]{:S(2)}, u32[]{:S(2)}) collective-permute-start(bf16[2048,800]{0,1:T(8,128)(2,1)} %param.9), channel_id=1, source_target_pairs={{0,4},{4,0},{1,5},{5,1},{2,6},{6,2},{3,7},{7,3},{8,12},{12,8},{9,1... | collective-permute-start | bytes 9830408 | tf_op jit(solution)/shard_map/ppermute | solution.py:14
  16.4 45.1 %copy-start = (bf16[512,1024]{1,0:T(8,128)(2,1)S(1)}, bf16[512,1024]{1,0:T(8,128)(2,1)}, u32[]{:S(2)}) copy-start(bf16[512,1024]{1,0:T(8,128)(2,1)} %param.7) | copy-start | bytes 3145732
  27.8 75.0 %collective-permute-start.5 = (bf16[513,1024]{1,0:T(8,128)(2,1)}, bf16[513,1024]{1,0:T(8,128)(2,1)S(1)}, u32[]{:S(2)}, u32[]{:S(2)}) collective-permute-start(bf16[513,1024]{1,0:T(8,128)(2,1)} %maximum_maximum_fusion), channel_id=1, source_target_pairs={{0,16},{8,24},{16,0},{24,8},{1,17},{9,25},{17,1},{25,9},{2,18},{10... | collective-permute-start | bytes 3151880 | tf_op jit(solution)/shard_map/ppermute | solution.py:29
  58.0 44.8 %collective-permute-start.6 = (bf16[512,1024]{1,0:T(8,128)(2,1)S(1)}, bf16[512,1024]{1,0:T(8,128)(2,1)S(1)}, u32[]{:S(2)}, u32[]{:S(2)}) collective-permute-start(bf16[512,1024]{1,0:T(8,128)(2,1)S(1)} %slice.145), channel_id=1, source_target_pairs={{0,1},{1,0},{2,3},{3,2},{4,5},{5,4},{6,7},{7,6},{8,9},{9,8},{10,11... | collective-permute-start | bytes 3145736 | tf_op jit(solution)/shard_map/ppermute | solution.py:14
  59.9 45.1 %collective-permute-start.7 = (bf16[512,1024]{1,0:T(8,128)(2,1)S(1)}, bf16[512,1024]{1,0:T(8,128)(2,1)S(1)}, u32[]{:S(2)}, u32[]{:S(2)}) collective-permute-start(bf16[512,1024]{1,0:T(8,128)(2,1)S(1)} %slice.146), channel_id=1, source_target_pairs={{0,1},{1,0},{2,3},{3,2},{4,5},{5,4},{6,7},{7,6},{8,9},{9,8},{10,11... | collective-permute-start | bytes 3145736 | tf_op jit(solution)/shard_map/ppermute | solution.py:14
  64.0 5.4 %copy-start.1 = (s32[512]{0:T(512)S(1)}, s32[512]{0:T(512)}, u32[]{:S(2)}) copy-start(s32[512]{0:T(512)} %param.10) | copy-start | bytes 6148
  88.8 40.6 %collective-permute-start.8 = (bf16[2048,800]{0,1:T(8,128)(2,1)}, bf16[2048,800]{0,1:T(8,128)(2,1)S(1)}, u32[]{:S(2)}, u32[]{:S(2)}) collective-permute-start(bf16[2048,800]{0,1:T(8,128)(2,1)} %collective-permute-done.4), channel_id=1, source_target_pairs={{0,2},{2,0},{1,3},{3,1},{4,6},{6,4},{5,7},{7,5},{8,10},{10,8},{9,1... | collective-permute-start | bytes 9830408 | tf_op jit(solution)/shard_map/ppermute | solution.py:14
  105.8 23.6 %collective-permute-start.9 = (bf16[512,1024]{1,0:T(8,128)(2,1)S(1)}, bf16[512,1024]{1,0:T(8,128)(2,1)S(1)}, u32[]{:S(2)}, u32[]{:S(2)}) collective-permute-start(bf16[512,1024]{1,0:T(8,128)(2,1)S(1)} %slice.150), channel_id=1, source_target_pairs={{0,1},{1,0},{2,3},{3,2},{4,5},{5,4},{6,7},{7,6},{8,9},{9,8},{10,11... | collective-permute-start | bytes 3145736 | tf_op jit(solution)/shard_map/ppermute | solution.py:14
  152.0 8.2 %copy-start.5 = (s32[16]{0:T(128)S(1)}, s32[16]{0:T(128)}, u32[]{:S(2)}) copy-start(s32[16]{0:T(128)} %param.13) | copy-start | bytes 196
  152.0 14.9 %copy-start.4 = (s32[512]{0:T(512)S(1)}, s32[512]{0:T(512)}, u32[]{:S(2)}) copy-start(s32[512]{0:T(512)} %param.11) | copy-start | bytes 6148
  156.5 10.3 %all-to-all-start = ((f32[8,4,256]{2,1,0:T(4,128)}), f32[8,4,256]{2,1,0:T(4,128)S(1)}, u32[]{:S(2)}, u32[]{:S(2)}) async-start(f32[8,4,256]{2,1,0:T(4,128)} %reshape.319), calls=%async_computation | async-start | bytes 65536 | tf_op jit(solution)/shard_map/all_to_all | solution.py:156
  167.0 12.0 %copy-start.3 = (f32[256]{0:T(256)}, f32[256]{0:T(256)S(1)}, u32[]{:S(2)}) copy-start(f32[256]{0:T(256)S(1)} %get-tuple-element.90) | copy-start | bytes 3076
  167.0 12.0 %copy-start.2 = (f32[256]{0:T(256)}, f32[256]{0:T(256)S(1)}, u32[]{:S(2)}) copy-start(f32[256]{0:T(256)S(1)} %subtract_multiply_fusion.1) | copy-start | bytes 3076

commit v2 on v1

--- a/solution.py
+++ b/solution.py
@@ -128,12 +128,20 @@
         for s in near[1:]:
             early[s] = [block_stats(values[s], rows[s][1], w, c) for w, c in held]
         pieces = held + ((w_d, cols[3]),)
+        blocks = []
         for s in range(n):
             if s in early:
                 parts = early[s] + [block_stats(values[s], rows[s][1], w_d, cols[3])]
             else:
                 parts = [block_stats(values[s], rows[s][1], w, c) for w, c in pieces]
-            stats.append(combine(parts))
+            blocks.append(jnp.stack(parts))
+        got = jnp.stack(blocks)
+        tops, totals, spreads, pickeds = got[:, :, 0], got[:, :, 1], got[:, :, 2], got[:, :, 3]
+        top = jnp.max(tops, axis=1)
+        scale = jnp.exp(tops - top[:, None, :])
+        total = jnp.sum(totals * scale, axis=1)
+        spread = jnp.sum(scale * (spreads + totals * (tops - top[:, None, :])), axis=1)
+        stats = jnp.stack([top, total, spread, jnp.sum(pickeds, axis=1)], axis=1)
     else:
         w_pair = jnp.concatenate([head_weight, w_p], 1)
         w_all = jnp.concatenate([w_pair, swap(w_pair, "dl")], 1)
@@ -149,7 +157,7 @@
                 h_s, t_s = moved[s - 1], moved_t[s - 1]
                 values = whole_rows(h_s, t, nt)
             stats.append(block_stats(values, t_s, w_all))
-    stats = jnp.stack(stats)
+    stats = jnp.stack(stats) if isinstance(stats, list) else stats
     stats = jnp.take(stats, (dh - jnp.arange(n)) % n, axis=0)
     rq = rb // nt
     stats = stats.reshape(n, 4, nt, rq).transpose(0, 2, 1, 3).reshape(n * nt, 4, rq)

time: 182 us -> 183 us (level)
    reduce_sum x4 -> x3, other arithmetic: 4.15 us -> 4.43 us  [normalize(): square = jnp.mean(values * values, axis=1, keepdims=True)]
where the time goes in v2:
time: 183 us; the launch traced here: 182 us
  waiting for transfers between devices  76.9 us (42%)
  matrix products  44.4 us (24%)
  other arithmetic  20.8 us (11%)
  starting transfers between devices  17.4 us (10%)
  blocking collectives  8.97 us (5%)
  local copies, waits for them, and re-layouts  8.01 us (4%)
  between operations  5.36 us (3%)
    dot_general x12, matrix products, block_stats(): jnp.dot(normalize(values), w_all, preferred_element_type=jnp.float32)  44.4 us
    ppermute x3, waiting for transfers between devices, shifted(): return lax.ppermute(x, 'dh', [(i, (i + s) % n) for i in range(n)])  39.2 us
    ppermute x7, waiting for transfers between devices, swap(): return lax.ppermute(x, name, [(0, 1), (1, 0)])  31.1 us
    reduce_sum x6, other arithmetic, block_stats(): total = jnp.sum(expo, axis=1)  10.5 us
    all_to_all x1, blocking collectives, per_device(): sums = jnp.sum(lax.all_to_all(parts, ALL, 0, 0, tiled=True), axis=0)  8.97 us
    ppermute x7, starting transfers between devices, swap(): return lax.ppermute(x, name, [(0, 1), (1, 0)])  7.43 us
    ppermute x3, starting transfers between devices, shifted(): return lax.ppermute(x, 'dh', [(i, (i + s) % n) for i in range(n)])  6.68 us
    all_to_all x1, waiting for transfers between devices, per_device(): got = lax.all_to_all(stats, ('dh', 't'), 0, 0, tiled=True)  6.54 us
  transfers between devices with their start and end apart: 11, of which 8 were waited for; matrix products, arithmetic and copies ran while one was open for 25% of the time, Pallas kernels for 0%

profile of v2, /device:TPU:0, one launch (start us, length us, event | category | flops | bytes accessed | tf_op | source)
XLA Modules:
  0.0 181.9 jit_solution(14652678357173814661)
XLA Ops:
  1.1 2.6 %collective-permute-start = (bf16[512,1024]{1,0:T(8,128)(2,1)}, bf16[512,1024]{1,0:T(8,128)(2,1)}, u32[]{:S(2)}, u32[]{:S(2)}) collective-permute-start(bf16[512,1024]{1,0:T(8,128)(2,1)} %param.7), channel_id=1, source_target_pairs={{0,1},{1,0},{2,3},{3,2},{4,5},{5,4},{6,7},{7,6},{8,9},{9,8},{10,11... | collective-permute-start | bytes 3145736 | tf_op jit(solution)/shard_map/ppermute | solution.py:14
  3.7 0.7 fusion.30
  4.4 2.3 %maximum_maximum_fusion = bf16[513,1024]{1,0:T(8,128)(2,1)} fusion(bf16[1,512]{1,0:T(2,128)(2,1)S(1)} %concatenate.56, bf16[1,512]{1,0:T(2,128)(2,1)S(1)} %concatenate.55, bf16[512,1024]{1,0:T(8,128)(2,1)} %param.7), kind=kLoop, calls=%fused_computation.73 | loop fusion | flops 3151872 | bytes 2101248 | tf_op jit(solution)/shard_map/concatenate | solution.py:94
  6.7 1.6 collective-permute-start.2
  8.3 2.2 %collective-permute-start.3 = (bf16[513,1024]{1,0:T(8,128)(2,1)}, bf16[513,1024]{1,0:T(8,128)(2,1)}, u32[]{:S(2)}, u32[]{:S(2)}) collective-permute-start(bf16[513,1024]{1,0:T(8,128)(2,1)} %maximum_maximum_fusion), channel_id=1, source_target_pairs={{0,24},{8,0},{16,8},{24,16},{1,25},{9,1},{17,9},{25,17},{2,26},{10... | collective-permute-start | bytes 3151880 | tf_op jit(solution)/shard_map/ppermute | solution.py:29
  10.5 1.5 collective-permute-start.4
  12.1 0.7 convert_element_type.70
  12.7 0.7 copy.51
  14.1 2.3 %constant_dynamic-update-slice_fusion.1 = bf16[2048,1600]{0,1:T(8,128)(2,1)S(1)} fusion(bf16[2048,800]{0,1:T(8,128)(2,1)} %param.9), kind=kLoop, calls=%fused_computation.117 | loop fusion | bytes 6553600
  16.4 11.4 %collective-permute-done = bf16[512,1024]{1,0:T(8,128)(2,1)} collective-permute-done((bf16[512,1024]{1,0:T(8,128)(2,1)}, bf16[512,1024]{1,0:T(8,128)(2,1)}, u32[]{:S(2)}, u32[]{:S(2)}) %collective-permute-start) | collective-permute-done | bytes 1048608 | tf_op jit(solution)/shard_map/ppermute | solution.py:14
  27.8 2.9 %collective-permute-start.5 = (bf16[513,1024]{1,0:T(8,128)(2,1)}, bf16[513,1024]{1,0:T(8,128)(2,1)S(1)}, u32[]{:S(2)}, u32[]{:S(2)}) collective-permute-start(bf16[513,1024]{1,0:T(8,128)(2,1)} %maximum_maximum_fusion), channel_id=1, source_target_pairs={{0,16},{8,24},{16,0},{24,8},{1,17},{9,25},{17,1},{25,9},{2,18},{10... | collective-permute-start | bytes 3151880 | tf_op jit(solution)/shard_map/ppermute | solution.py:29
  30.6 4.6 %collective-permute-done.2 = bf16[513,1024]{1,0:T(8,128)(2,1)} collective-permute-done((bf16[513,1024]{1,0:T(8,128)(2,1)}, bf16[513,1024]{1,0:T(8,128)(2,1)}, u32[]{:S(2)}, u32[]{:S(2)}) %collective-permute-start.2) | collective-permute-done | bytes 1050656 | tf_op jit(solution)/shard_map/ppermute | solution.py:29
  35.2 21.5 %collective-permute-done.3 = bf16[513,1024]{1,0:T(8,128)(2,1)} collective-permute-done((bf16[513,1024]{1,0:T(8,128)(2,1)}, bf16[513,1024]{1,0:T(8,128)(2,1)}, u32[]{:S(2)}, u32[]{:S(2)}) %collective-permute-start.3) | collective-permute-done | bytes 1050656 | tf_op jit(solution)/shard_map/ppermute | solution.py:29
  56.7 1.3 slice.109
  58.0 0.6 collective-permute-start.6
  58.6 1.3 slice.110
  59.9 1.6 collective-permute-start.7
  61.5 2.3 %fusion = f32[512]{0:T(512)S(1)} fusion(bf16[512,1024]{1,0:T(8,128)(2,1)S(1)} %copy-done, bf16[512,1024]{1,0:T(8,128)(2,1)} %collective-permute-done, pred[]{:T(512)S(6)} %eq.65), kind=kLoop, calls=%fused_computation.17 | loop fusion | flops 12582400 | bytes 2099201 | tf_op jit(solution)/shard_map/reduce_sum | solution.py:64
  64.0 5.4 %fusion.63 = (f32[512]{0:T(512)S(1)}, f32[512,1600]{0,1:T(8,128)S(1)}) fusion(bf16[2048,1600]{0,1:T(8,128)(2,1)S(1)} %constant_dynamic-update-slice_fusion, f32[2048]{0:T(1024)S(1)} %convert_element_type.70, f32[512]{0:T(512)S(1)} %add_rsqrt_fusion.3, bf16[512,1024]{1,0:T(8,128)(2,1)S(1)} %copy-done, bf16[512,1024]{1,0:T(8,128)(2,1)} %collective-permute-done, ...), kind=kOutput, calls=%fused_computation.180 | convolution fusion | flops 3369893376 | bytes 11939841 | tf_op jit(solution)/shard_map/dot_general | solution.py:69
  69.5 1.6 exponential_reduce_fusion.3
  71.1 12.3 %collective-permute-done.4 = bf16[2048,800]{0,1:T(8,128)(2,1)} collective-permute-done((bf16[2048,800]{0,1:T(8,128)(2,1)}, bf16[2048,800]{0,1:T(8,128)(2,1)}, u32[]{:S(2)}, u32[]{:S(2)}) %collective-permute-start.4) | collective-permute-done | bytes 3276832 | tf_op jit(solution)/shard_map/ppermute | solution.py:14
  83.3 5.0 %fusion.64 = (f32[512]{0:T(512)S(1)}, f32[512,800]{0,1:T(8,128)S(1)}) fusion(bf16[2048,800]{0,1:T(8,128)(2,1)} %collective-permute-done.4, f32[2048]{0:T(1024)S(1)} %convert_element_type.70, f32[512]{0:T(512)S(1)} %add_rsqrt_fusion.3, bf16[512,1024]{1,0:T(8,128)(2,1)S(1)} %copy-done, bf16[512,1024]{1,0:T(8,128)(2,1)} %collective-permute-done, pred[]{:T(512)S(6)} %eq.65), kind=kOutput, calls=%fused_computation.181 | convolution fusion | flops 1691762176 | bytes 7024641 | tf_op jit(solution)/shard_map/dot_general | solution.py:69
  88.9 0.7 slice_convert_fusion
  89.7 13.1 %collective-permute-done.5 = bf16[513,1024]{1,0:T(8,128)(2,1)S(1)} collective-permute-done((bf16[513,1024]{1,0:T(8,128)(2,1)}, bf16[513,1024]{1,0:T(8,128)(2,1)S(1)}, u32[]{:S(2)}, u32[]{:S(2)}) %collective-permute-start.5) | collective-permute-done | bytes 1050656 | tf_op jit(solution)/shard_map/ppermute | solution.py:29
  102.8 2.2 %collective-permute-done.7 = bf16[512,1024]{1,0:T(8,128)(2,1)S(1)} collective-permute-done((bf16[512,1024]{1,0:T(8,128)(2,1)S(1)}, bf16[512,1024]{1,0:T(8,128)(2,1)S(1)}, u32[]{:S(2)}, u32[]{:S(2)}) %collective-permute-start.7) | collective-permute-done | bytes 1048608 | tf_op jit(solution)/shard_map/ppermute | solution.py:14
  105.2 1.5 fusion.3
  106.7 0.6 collective-permute-start.9
  107.3 4.0 %fusion.66 = (f32[512]{0:T(512)S(1)}, f32[512,800]{0,1:T(8,128)S(1)}) fusion(bf16[2048,800]{0,1:T(8,128)(2,1)} %collective-permute-done.4, f32[512]{0:T(512)S(1)} %add_rsqrt_fusion.2, f32[2048]{0:T(1024)S(1)} %convert_element_type.70, bf16[512,1024]{1,0:T(8,128)(2,1)S(1)} %slice.109, bf16[512,1024]{1,0:T(8,128)(2,1)S(1)} %collective-permute-done.6, ...), kind=kOutput, calls=%fused_computation.183 | convolution fusion | flops 1691762176 | bytes 7024641 | tf_op jit(solution)/shard_map/dot_general | solution.py:69
  111.8 3.8 %fusion.65 = (f32[512]{0:T(512)S(1)}, f32[512,1600]{0,1:T(8,128)S(1)}) fusion(bf16[2048,1600]{0,1:T(8,128)(2,1)S(1)} %constant_dynamic-update-slice_fusion, f32[512]{0:T(512)S(1)} %add_rsqrt_fusion.2, f32[2048]{0:T(1024)S(1)} %convert_element_type.70, bf16[512,1024]{1,0:T(8,128)(2,1)S(1)} %slice.109, bf16[512,1024]{1,0:T(8,128)(2,1)S(1)} %collective-permute-done.6, ...), kind=kOutput, calls=%fused_computation.182 | convolution fusion | flops 3369893376 | bytes 11939841 | tf_op jit(solution)/shard_map/dot_general | solution.py:69
  115.6 1.6 exponential_reduce_fusion.2
  117.3 4.0 %fusion.71 = (f32[512]{0:T(512)S(1)}, f32[512,800]{0,1:T(8,128)S(1)}) fusion(bf16[2048,800]{0,1:T(8,128)(2,1)} %collective-permute-done.4, f32[512]{0:T(512)S(1)} %add_rsqrt_fusion, f32[2048]{0:T(1024)S(1)} %convert_element_type.70, bf16[512,1024]{1,0:T(8,128)(2,1)S(1)} %slice.110, bf16[512,1024]{1,0:T(8,128)(2,1)S(1)} %collective-permute-done.7, pred[]{:T(512)S(6)} %eq.65), kind=kOutput, calls=%fused_computation.188 | convolution fusion | flops 1691762176 | bytes 7024641 | tf_op jit(solution)/shard_map/dot_general | solution.py:69
  121.3 3.8 %fusion.74 = (f32[512]{0:T(512)S(1)}, f32[512,1600]{0,1:T(8,128)S(1)}) fusion(bf16[2048,1600]{0,1:T(8,128)(2,1)S(1)} %constant_dynamic-update-slice_fusion, f32[512]{0:T(512)S(1)} %add_rsqrt_fusion, f32[2048]{0:T(1024)S(1)} %convert_element_type.70, bf16[512,1024]{1,0:T(8,128)(2,1)S(1)} %slice.110, bf16[512,1024]{1,0:T(8,128)(2,1)S(1)} %collective-permute-done.7, ...), kind=kOutput, calls=%fused_computation.191 | convolution fusion | flops 3369893376 | bytes 11939841 | tf_op jit(solution)/shard_map/dot_general | solution.py:69
  125.2 5.2 %collective-permute-done.9 = bf16[512,1024]{1,0:T(8,128)(2,1)S(1)} collective-permute-done((bf16[512,1024]{1,0:T(8,128)(2,1)S(1)}, bf16[512,1024]{1,0:T(8,128)(2,1)S(1)}, u32[]{:S(2)}, u32[]{:S(2)}) %collective-permute-start.9) | collective-permute-done | bytes 1048608 | tf_op jit(solution)/shard_map/ppermute | solution.py:14
  130.3 4.5 %fusion.67 = (f32[512]{0:T(512)S(1)}, f32[512,800]{0,1:T(8,128)S(1)}) fusion(bf16[2048,800]{0,1:T(8,128)(2,1)S(1)} %collective-permute-done.8, f32[2048]{0:T(1024)S(1)} %convert_element_type.70, f32[512]{0:T(512)S(1)} %add_rsqrt_fusion.3, bf16[512,1024]{1,0:T(8,128)(2,1)S(1)} %copy-done, bf16[512,1024]{1,0:T(8,128)(2,1)} %collective-permute-done, pred[]{:T(512)S(6)} %eq.65), kind=kOutput, calls=%fused_computation.184 | convolution fusion | flops 1691762176 | bytes 7024641 | tf_op jit(solution)/shard_map/dot_general | solution.py:69
  134.8 2.1 %fusion.68 = (f32[512]{0:T(512)S(1)}, f32[512,800]{0,1:T(8,128)S(1)}) fusion(bf16[2048,800]{0,1:T(8,128)(2,1)S(1)} %collective-permute-done.8, f32[512]{0:T(512)S(1)} %add_rsqrt_fusion.2, f32[2048]{0:T(1024)S(1)} %convert_element_type.70, bf16[512,1024]{1,0:T(8,128)(2,1)S(1)} %slice.109, bf16[512,1024]{1,0:T(8,128)(2,1)S(1)} %collective-permute-done.6, ...), kind=kOutput, calls=%fused_computation.185 | convolution fusion | flops 1691762176 | bytes 7024641 | tf_op jit(solution)/shard_map/dot_general | solution.py:69
  136.9 2.1 %fusion.70 = (f32[512]{0:T(512)S(1)}, f32[512,800]{0,1:T(8,128)S(1)}) fusion(bf16[2048,800]{0,1:T(8,128)(2,1)S(1)} %collective-permute-done.8, f32[512]{0:T(512)S(1)} %add_rsqrt_fusion, f32[2048]{0:T(1024)S(1)} %convert_element_type.70, bf16[512,1024]{1,0:T(8,128)(2,1)S(1)} %slice.110, bf16[512,1024]{1,0:T(8,128)(2,1)S(1)} %collective-permute-done.7, ...), kind=kOutput, calls=%fused_computation.187 | convolution fusion | flops 1691762176 | bytes 7024641 | tf_op jit(solution)/shard_map/dot_general | solution.py:69
  138.9 0.6 fusion.6
  139.6 2.1 %fusion.69 = (f32[512]{0:T(512)S(1)}, f32[512,800]{0,1:T(8,128)S(1)}) fusion(bf16[2048,800]{0,1:T(8,128)(2,1)S(1)} %collective-permute-done.8, f32[512]{0:T(512)S(1)} %add_rsqrt_fusion.1, f32[2048]{0:T(1024)S(1)} %convert_element_type.70, bf16[512,1024]{1,0:T(8,128)(2,1)S(1)} %slice.114, bf16[512,1024]{1,0:T(8,128)(2,1)S(1)} %collective-permute-done.9, ...), kind=kOutput, calls=%fused_computation.186 | convolution fusion | flops 1691762176 | bytes 7024641 | tf_op jit(solution)/shard_map/dot_general | solution.py:69
  141.6 3.8 %fusion.73 = (f32[512]{0:T(512)S(1)}, f32[512,1600]{0,1:T(8,128)S(1)}) fusion(bf16[2048,1600]{0,1:T(8,128)(2,1)S(1)} %constant_dynamic-update-slice_fusion, f32[512]{0:T(512)S(1)} %add_rsqrt_fusion.1, f32[2048]{0:T(1024)S(1)} %convert_element_type.70, bf16[512,1024]{1,0:T(8,128)(2,1)S(1)} %slice.114, bf16[512,1024]{1,0:T(8,128)(2,1)S(1)} %collective-permute-done.9, ...), kind=kOutput, calls=%fused_computation.190 | convolution fusion | flops 3369893376 | bytes 11939841 | tf_op jit(solution)/shard_map/dot_general | solution.py:69
  145.4 4.0 %fusion.72 = (f32[512]{0:T(512)S(1)}, f32[512,800]{0,1:T(8,128)S(1)}) fusion(bf16[2048,800]{0,1:T(8,128)(2,1)} %collective-permute-done.4, f32[512]{0:T(512)S(1)} %add_rsqrt_fusion.1, f32[2048]{0:T(1024)S(1)} %convert_element_type.70, bf16[512,1024]{1,0:T(8,128)(2,1)S(1)} %slice.114, bf16[512,1024]{1,0:T(8,128)(2,1)S(1)} %collective-permute-done.9, ...), kind=kOutput, calls=%fused_computation.189 | convolution fusion | flops 1691762176 | bytes 7024641 | tf_op jit(solution)/shard_map/dot_general | solution.py:69
  149.4 3.6 %exponential_reduce_fusion.9 = (f32[512]{0:T(512)S(1)}, f32[512]{0:T(512)S(1)}, f32[512]{0:T(512)S(1)}, f32[512]{0:T(512)S(1)}, f32[512]{0:T(512)S(1)}, /*index=...) fusion(f32[512,800]{0,1:T(8,128)S(1)} %get-tuple-element.123, ...), kind=kLoop, calls=%fused_computation.48 | loop fusion | flops 17193984 | bytes 9894144 | tf_op jit(solution)/shard_map/reduce_sum | solution.py:73
  153.1 2.6 %exponential_reduce_fusion.1 = (f32[512]{0:T(512)S(1)}, f32[512]{0:T(512)S(1)}, f32[512]{0:T(512)S(1)}, f32[512]{0:T(512)S(1)}, f32[512]{0:T(512)S(1)}, /*index=5*/f32[512]{0:T(512)S(1)}) fusion(f32[512,1600]{0,1:T(8,128)S(1)} %get-tuple-element.135, f32[512]{0:T(512)S(1)} %get-tuple-element.134, s32[512]{0:T(512)S(1)} %bitcast.157, ...), kind=kLoop, calls=%fused_computation.12 | loop fusion | flops 11465728 | bytes 6580480 | tf_op jit(solution)/shard_map/reduce_sum | solution.py:73
  156.3 0.6 gather_fusion
  156.9 0.6 reshape.316
  157.6 3.3 %all-to-all-start = ((f32[8,4,256]{2,1,0:T(4,128)}), f32[8,4,256]{2,1,0:T(4,128)S(1)}, u32[]{:S(2)}, u32[]{:S(2)}) async-start(f32[8,4,256]{2,1,0:T(4,128)} %reshape.316), calls=%async_computation | async-start | bytes 65536 | tf_op jit(solution)/shard_map/all_to_all | solution.py:164
  161.0 6.5 %all-to-all-done = f32[8,4,256]{2,1,0:T(4,128)S(1)} async-done(((f32[8,4,256]{2,1,0:T(4,128)}), f32[8,4,256]{2,1,0:T(4,128)S(1)}, u32[]{:S(2)}, u32[]{:S(2)}) %all-to-all-start) | async-done | bytes 32800 | tf_op jit(solution)/shard_map/all_to_all | solution.py:164
  167.9 9.0 %all_to_all.10 = f32[32,3,1]{1,2,0:T(1,128)S(1)} all-to-all(f32[32,3,1]{1,2,0:T(1,128)S(1)} %bitcast.146), channel_id=1, replica_groups=mesh['dh'=4,'p'=2,'dl'=2,'t'=2] {'dh','p','dl','t'}, dimensions={0} | all-to-all | bytes 768 | tf_op jit(solution)/shard_map/all_to_all | solution.py:187
  176.9 0.7 fusion.62
  (79 shorter events, 3.6 us)
Async XLA Ops:
  0.6 56.1 %collective-permute-start.1 = (bf16[2048,800]{0,1:T(8,128)(2,1)}, bf16[2048,800]{0,1:T(8,128)(2,1)S(1)}, u32[]{:S(2)}, u32[]{:S(2)}) collective-permute-start(bf16[2048,800]{0,1:T(8,128)(2,1)} %param.9), channel_id=1, source_target_pairs={{0,2},{2,0},{1,3},{3,1},{4,6},{6,4},{5,7},{7,5},{8,10},{10,8},{9,1... | collective-permute-start | bytes 9830408 | tf_op jit(solution)/shard_map/ppermute | solution.py:14
  1.1 26.6 %collective-permute-start = (bf16[512,1024]{1,0:T(8,128)(2,1)}, bf16[512,1024]{1,0:T(8,128)(2,1)}, u32[]{:S(2)}, u32[]{:S(2)}) collective-permute-start(bf16[512,1024]{1,0:T(8,128)(2,1)} %param.7), channel_id=1, source_target_pairs={{0,1},{1,0},{2,3},{3,2},{4,5},{5,4},{6,7},{7,6},{8,9},{9,8},{10,11... | collective-permute-start | bytes 3145736 | tf_op jit(solution)/shard_map/ppermute | solution.py:14
  6.7 28.5 %collective-permute-start.2 = (bf16[513,1024]{1,0:T(8,128)(2,1)}, bf16[513,1024]{1,0:T(8,128)(2,1)}, u32[]{:S(2)}, u32[]{:S(2)}) collective-permute-start(bf16[513,1024]{1,0:T(8,128)(2,1)} %maximum_maximum_fusion), channel_id=1, source_target_pairs={{0,8},{8,16},{16,24},{24,0},{1,9},{9,17},{17,25},{25,1},{2,10},{10... | collective-permute-start | bytes 3151880 | tf_op jit(solution)/shard_map/ppermute | solution.py:29
  8.3 48.4 %collective-permute-start.3 = (bf16[513,1024]{1,0:T(8,128)(2,1)}, bf16[513,1024]{1,0:T(8,128)(2,1)}, u32[]{:S(2)}, u32[]{:S(2)}) collective-permute-start(bf16[513,1024]{1,0:T(8,128)(2,1)} %maximum_maximum_fusion), channel_id=1, source_target_pairs={{0,24},{8,0},{16,8},{24,16},{1,25},{9,1},{17,9},{25,17},{2,26},{10... | collective-permute-start | bytes 3151880 | tf_op jit(solution)/shard_map/ppermute | solution.py:29
  10.5 72.8 %collective-permute-start.4 = (bf16[2048,800]{0,1:T(8,128)(2,1)}, bf16[2048,800]{0,1:T(8,128)(2,1)}, u32[]{:S(2)}, u32[]{:S(2)}) collective-permute-start(bf16[2048,800]{0,1:T(8,128)(2,1)} %param.9), channel_id=1, source_target_pairs={{0,4},{4,0},{1,5},{5,1},{2,6},{6,2},{3,7},{7,3},{8,12},{12,8},{9,1... | collective-permute-start | bytes 9830408 | tf_op jit(solution)/shard_map/ppermute | solution.py:14
  16.4 45.1 %copy-start = (bf16[512,1024]{1,0:T(8,128)(2,1)S(1)}, bf16[512,1024]{1,0:T(8,128)(2,1)}, u32[]{:S(2)}) copy-start(bf16[512,1024]{1,0:T(8,128)(2,1)} %param.7) | copy-start | bytes 3145732
  27.8 75.0 %collective-permute-start.5 = (bf16[513,1024]{1,0:T(8,128)(2,1)}, bf16[513,1024]{1,0:T(8,128)(2,1)S(1)}, u32[]{:S(2)}, u32[]{:S(2)}) collective-permute-start(bf16[513,1024]{1,0:T(8,128)(2,1)} %maximum_maximum_fusion), channel_id=1, source_target_pairs={{0,16},{8,24},{16,0},{24,8},{1,17},{9,25},{17,1},{25,9},{2,18},{10... | collective-permute-start | bytes 3151880 | tf_op jit(solution)/shard_map/ppermute | solution.py:29
  58.0 44.8 %collective-permute-start.6 = (bf16[512,1024]{1,0:T(8,128)(2,1)S(1)}, bf16[512,1024]{1,0:T(8,128)(2,1)S(1)}, u32[]{:S(2)}, u32[]{:S(2)}) collective-permute-start(bf16[512,1024]{1,0:T(8,128)(2,1)S(1)} %slice.109), channel_id=1, source_target_pairs={{0,1},{1,0},{2,3},{3,2},{4,5},{5,4},{6,7},{7,6},{8,9},{9,8},{10,11... | collective-permute-start | bytes 3145736 | tf_op jit(solution)/shard_map/ppermute | solution.py:14
  59.9 45.1 %collective-permute-start.7 = (bf16[512,1024]{1,0:T(8,128)(2,1)S(1)}, bf16[512,1024]{1,0:T(8,128)(2,1)S(1)}, u32[]{:S(2)}, u32[]{:S(2)}) collective-permute-start(bf16[512,1024]{1,0:T(8,128)(2,1)S(1)} %slice.110), channel_id=1, source_target_pairs={{0,1},{1,0},{2,3},{3,2},{4,5},{5,4},{6,7},{7,6},{8,9},{9,8},{10,11... | collective-permute-start | bytes 3145736 | tf_op jit(solution)/shard_map/ppermute | solution.py:14
  64.0 5.4 %copy-start.1 = (s32[512]{0:T(512)S(1)}, s32[512]{0:T(512)}, u32[]{:S(2)}) copy-start(s32[512]{0:T(512)} %param.10) | copy-start | bytes 6148
  88.3 42.0 %collective-permute-start.8 = (bf16[2048,800]{0,1:T(8,128)(2,1)}, bf16[2048,800]{0,1:T(8,128)(2,1)S(1)}, u32[]{:S(2)}, u32[]{:S(2)}) collective-permute-start(bf16[2048,800]{0,1:T(8,128)(2,1)} %collective-permute-done.4), channel_id=1, source_target_pairs={{0,2},{2,0},{1,3},{3,1},{4,6},{6,4},{5,7},{7,5},{8,10},{10,8},{9,1... | collective-permute-start | bytes 9830408 | tf_op jit(solution)/shard_map/ppermute | solution.py:14
  106.7 23.6 %collective-permute-start.9 = (bf16[512,1024]{1,0:T(8,128)(2,1)S(1)}, bf16[512,1024]{1,0:T(8,128)(2,1)S(1)}, u32[]{:S(2)}, u32[]{:S(2)}) collective-permute-start(bf16[512,1024]{1,0:T(8,128)(2,1)S(1)} %slice.114), channel_id=1, source_target_pairs={{0,1},{1,0},{2,3},{3,2},{4,5},{5,4},{6,7},{7,6},{8,9},{9,8},{10,11... | collective-permute-start | bytes 3145736 | tf_op jit(solution)/shard_map/ppermute | solution.py:14
  153.1 7.8 %copy-start.5 = (s32[16]{0:T(128)S(1)}, s32[16]{0:T(128)}, u32[]{:S(2)}) copy-start(s32[16]{0:T(128)} %param.13) | copy-start | bytes 196
  153.1 14.5 %copy-start.4 = (s32[512]{0:T(512)S(1)}, s32[512]{0:T(512)}, u32[]{:S(2)}) copy-start(s32[512]{0:T(512)} %param.11) | copy-start | bytes 6148
  157.6 10.0 %all-to-all-start = ((f32[8,4,256]{2,1,0:T(4,128)}), f32[8,4,256]{2,1,0:T(4,128)S(1)}, u32[]{:S(2)}, u32[]{:S(2)}) async-start(f32[8,4,256]{2,1,0:T(4,128)} %reshape.316), calls=%async_computation | async-start | bytes 65536 | tf_op jit(solution)/shard_map/all_to_all | solution.py:164
  167.7 11.9 %copy-start.3 = (f32[256]{0:T(256)}, f32[256]{0:T(256)S(1)}, u32[]{:S(2)}) copy-start(f32[256]{0:T(256)S(1)} %get-tuple-element.78) | copy-start | bytes 3076
  167.7 11.9 %copy-start.2 = (f32[256]{0:T(256)}, f32[256]{0:T(256)S(1)}, u32[]{:S(2)}) copy-start(f32[256]{0:T(256)S(1)} %subtract_multiply_fusion.1) | copy-start | bytes 3076

commit v3 on v1

--- a/solution.py
+++ b/solution.py
@@ -91,17 +91,20 @@
     if n <= 4 and fast:
         extra = (2 * rb) // dt
         code = jnp.concatenate([target_ids // 128, target_ids % 128]).astype(jnp.bfloat16).reshape(extra, dt)
-        carried = jnp.concatenate([hidden_states, code], 0)
         near = [s for s in sorted({1, n - 1}) if 1 <= s < n]
         far = [s for s in range(1, n) if s not in near]
         cols = [column[i * cb:(i + 1) * cb] for i in range(4)]
 
-        def unpack(block):
-            parts = block[rb:].reshape(2, rb).astype(jnp.int32)
-            return block[:rb], parts[0] * 128 + parts[1]
+        def unpack(pair):
+            block, coded = pair
+            parts = coded.reshape(2, rb).astype(jnp.int32)
+            return block, parts[0] * 128 + parts[1]
+
+        def moved(s):
+            return (shifted(hidden_states, s, n, dh), shifted(code, s, n, dh))
 
         own_other, w_c, got = lax.optimization_barrier(
-            (swap(hidden_states, "t"), swap(head_weight, "dl"), [shifted(carried, s, n, dh) for s in near]))
+            (swap(hidden_states, "t"), swap(head_weight, "dl"), [moved(s) for s in near]))
         rows = {0: (hidden_states, target_ids)}
         for s, block in zip(near, got):
             rows[s] = unpack(block)
@@ -111,7 +114,7 @@
         held = ((w_own, c_own), (w_p, cols[1]))
         first = [block_stats(values[0], target_ids, w, c) for w, c in held]
         first, got, others = lax.optimization_barrier(
-            (first, [shifted(carried, s, n, dh) for s in far], [swap(rows[s][0], "t") for s in near]))
+            (first, [moved(s) for s in far], [swap(rows[s][0], "t") for s in near]))
         for s, block in zip(far, got):
             rows[s] = unpack(block)
         for s, other in zip(near, others):

time: 182 us -> 216 us (1.19)
  waiting for transfers between devices: 75.6 us -> 106 us
  matrix products: 44.2 us -> 49.3 us
  local copies, waits for them, and re-layouts: 7.98 us -> 5.41 us
    ppermute x7, waiting for transfers between devices: 30.5 us -> 53.6 us  [swap(): return lax.ppermute(x, name, [(0, 1), (1, 0)])]
    ppermute x3 -> x6, waiting for transfers between devices: 38.5 us -> 45.5 us  [shifted(): return lax.ppermute(x, 'dh', [(i, (i + s) % n) for i in range(n)])]
    dot_general x12, matrix products: 44.2 us -> 49.3 us  [block_stats(): jnp.dot(normalize(values), w_all, preferred_element_type=jnp.float32)]
    reduce_sum x4, other arithmetic: 4.15 us -> 7.46 us  [normalize(): square = jnp.mean(values * values, axis=1, keepdims=True)]
    slice x3 -> x0, local copies, waits for them, and re-layouts: 2.66 us -> none  [unpack(): return (block[:rb], parts[0] * 128 + parts[1])]
    concatenate x2 -> x1, other arithmetic: 2.3 us -> 0.01 us  [the longest x1 2.29 us: per_device(): carried = jnp.concatenate([hidden_states, code], 0)]
    ppermute x3 -> x6, starting transfers between devices: 6.68 us -> 8.56 us  [shifted(): return lax.ppermute(x, 'dh', [(i, (i + s) % n) for i in range(n)])]
  transfers between devices with their start and end apart: 11 -> 14, of which waited for: 8 -> 5; matrix products, arithmetic and copies ran while one was open for 25% -> 21% of each run, Pallas kernels for 0% -> 0%
where the time goes in v3:
time: 216 us; the launch traced here: 215 us
  waiting for transfers between devices  106 us (49%)
  matrix products  49.3 us (23%)
  other arithmetic  20.7 us (10%)
  starting transfers between devices  19.6 us (9%)
  blocking collectives  8.88 us (4%)
  local copies, waits for them, and re-layouts  5.41 us (3%)
  between operations  5.4 us (2%)
    ppermute x7, waiting for transfers between devices, swap(): return lax.ppermute(x, name, [(0, 1), (1, 0)])  53.6 us
    dot_general x12, matrix products, block_stats(): jnp.dot(normalize(values), w_all, preferred_element_type=jnp.float32)  49.3 us
    ppermute x6, waiting for transfers between devices, shifted(): return lax.ppermute(x, 'dh', [(i, (i + s) % n) for i in range(n)])  45.5 us
    reduce_sum x6, other arithmetic, block_stats(): total = jnp.sum(expo, axis=1)  10.3 us
    all_to_all x1, blocking collectives, per_device(): sums = jnp.sum(lax.all_to_all(parts, ALL, 0, 0, tiled=True), axis=0)  8.88 us
    ppermute x6, starting transfers between devices, shifted(): return lax.ppermute(x, 'dh', [(i, (i + s) % n) for i in range(n)])  8.56 us
    ppermute x7, starting transfers between devices, swap(): return lax.ppermute(x, name, [(0, 1), (1, 0)])  7.51 us
    reduce_sum x4, other arithmetic, normalize(): square = jnp.mean(values * values, axis=1, keepdims=True)  7.46 us
  transfers between devices with their start and end apart: 14, of which 5 were waited for; matrix products, arithmetic and copies ran while one was open for 21% of the time, Pallas kernels for 0%

profile of v3, /device:TPU:0, one launch (start us, length us, event | category | flops | bytes accessed | tf_op | source)
XLA Modules:
  0.0 215.0 jit_solution(5818358972786375321)
XLA Ops:
  0.6 0.5 collective-permute-start.1
  1.1 2.6 %collective-permute-start = (bf16[512,1024]{1,0:T(8,128)(2,1)}, bf16[512,1024]{1,0:T(8,128)(2,1)}, u32[]{:S(2)}, u32[]{:S(2)}) collective-permute-start(bf16[512,1024]{1,0:T(8,128)(2,1)} %param.7), channel_id=1, source_target_pairs={{0,1},{1,0},{2,3},{3,2},{4,5},{5,4},{6,7},{7,6},{8,9},{9,8},{10,11... | collective-permute-start | bytes 3145736 | tf_op jit(solution)/shard_map/ppermute | solution.py:14
  3.7 1.6 collective-permute-start.2
  5.3 2.2 %collective-permute-start.4 = (bf16[512,1024]{1,0:T(8,128)(2,1)}, bf16[512,1024]{1,0:T(8,128)(2,1)}, u32[]{:S(2)}, u32[]{:S(2)}) collective-permute-start(bf16[512,1024]{1,0:T(8,128)(2,1)} %param.7), channel_id=1, source_target_pairs={{0,24},{8,0},{16,8},{24,16},{1,25},{9,1},{17,9},{25,17},{2,26},{10... | collective-permute-start | bytes 3145736 | tf_op jit(solution)/shard_map/ppermute | solution.py:29
  7.5 0.7 fusion.60
  8.6 45.1 %collective-permute-done.3 = bf16[1,1024]{1,0:T(2,128)(2,1)S(1)} collective-permute-done((bf16[1,1024]{1,0:T(2,128)(2,1)S(1)}, bf16[1,1024]{1,0:T(2,128)(2,1)S(1)}, u32[]{:S(2)}, u32[]{:S(2)}) %collective-permute-start.3) | collective-permute-done | bytes 2080 | tf_op jit(solution)/shard_map/ppermute | solution.py:29
  53.7 1.7 collective-permute-start.5
  55.4 0.7 convert_element_type.70
  56.1 0.7 copy.74
  57.0 0.3 collective-permute-done.5
  57.3 1.5 collective-permute-start.6
  59.0 2.4 %constant_dynamic-update-slice_fusion.3 = bf16[2048,1600]{0,1:T(8,128)(2,1)S(1)} fusion(bf16[2048,800]{0,1:T(8,128)(2,1)} %param.9), kind=kLoop, calls=%fused_computation.87 | loop fusion | bytes 6553600
  61.4 0.7 collective-permute-start.7
  62.2 2.3 %collective-permute-start.8 = (bf16[1,1024]{1,0:T(2,128)(2,1)S(1)}, bf16[1,1024]{1,0:T(2,128)(2,1)S(1)}, u32[]{:S(2)}, u32[]{:S(2)}) collective-permute-start(bf16[1,1024]{1,0:T(2,128)(2,1)S(1)} %constant_dynamic-update-slice_fusion), channel_id=1, source_target_pairs={{0,16},{8,24},{16,0},{24,8},{1,17},{9,25},{17,1},{25,9},{2,18},{10... | collective-permute-start | bytes 6152 | tf_op jit(solution)/shard_map/ppermute | solution.py:29
  64.4 0.5 collective-permute-start.9
  65.0 1.5 collective-permute-start.10
  66.5 2.2 %fusion = f32[512]{0:T(512)S(1)} fusion(bf16[512,1024]{1,0:T(8,128)(2,1)S(1)} %copy-done, bf16[512,1024]{1,0:T(8,128)(2,1)} %collective-permute-done, pred[]{:T(512)S(6)} %eq.65), kind=kLoop, calls=%fused_computation.17 | loop fusion | flops 12582400 | bytes 2099201 | tf_op jit(solution)/shard_map/reduce_sum | solution.py:64
  68.7 0.2 constant_dynamic-update-slice_fusion.2
  69.0 5.4 %fusion.96 = (f32[512]{0:T(512)S(1)}, f32[512,1600]{0,1:T(8,128)S(1)}) fusion(bf16[2048,1600]{0,1:T(8,128)(2,1)S(1)} %constant_dynamic-update-slice_fusion.2, f32[2048]{0:T(1024)S(1)} %convert_element_type.70, f32[512]{0:T(512)S(1)} %add_rsqrt_fusion.3, bf16[512,1024]{1,0:T(8,128)(2,1)S(1)} %copy-done, bf16[512,1024]{1,0:T(8,128)(2,1)} %collective-permute-done, ...), kind=kOutput, calls=%fused_computation.224 | convolution fusion | flops 3369893376 | bytes 11939841 | tf_op jit(solution)/shard_map/dot_general | solution.py:69
  74.4 1.6 exponential_reduce_fusion.3
  76.0 52.3 %collective-permute-done.6 = bf16[2048,800]{0,1:T(8,128)(2,1)S(1)} collective-permute-done((bf16[2048,800]{0,1:T(8,128)(2,1)}, bf16[2048,800]{0,1:T(8,128)(2,1)S(1)}, u32[]{:S(2)}, u32[]{:S(2)}) %collective-permute-start.6) | collective-permute-done | bytes 3276832 | tf_op jit(solution)/shard_map/ppermute | solution.py:14
  128.3 4.1 %fusion.97 = (f32[512]{0:T(512)S(1)}, f32[512,800]{0,1:T(8,128)S(1)}) fusion(bf16[2048,800]{0,1:T(8,128)(2,1)S(1)} %collective-permute-done.6, f32[2048]{0:T(1024)S(1)} %convert_element_type.70, f32[512]{0:T(512)S(1)} %add_rsqrt_fusion.3, bf16[512,1024]{1,0:T(8,128)(2,1)S(1)} %copy-done, bf16[512,1024]{1,0:T(8,128)(2,1)} %collective-permute-done, pred[]{:T(512)S(6)} %eq.65), kind=kOutput, calls=%fused_computation.225 | convolution fusion | flops 1691762176 | bytes 7024641 | tf_op jit(solution)/shard_map/dot_general | solution.py:69
  132.4 0.5 exponential_reduce_fusion.11
  133.1 2.4 %fusion.3 = f32[512]{0:T(512)S(1)} fusion(bf16[512,1024]{1,0:T(8,128)(2,1)} %collective-permute-done.2, bf16[512,1024]{1,0:T(8,128)(2,1)S(1)} %collective-permute-done.9, pred[]{:T(512)S(6)} %eq.65), kind=kLoop, calls=%fused_computation.20 | loop fusion | flops 12582400 | bytes 2099201 | tf_op jit(solution)/shard_map/reduce_sum | solution.py:64
  135.4 0.8 collective-permute-start.12
  136.2 2.2 %fusion.9 = f32[512]{0:T(512)S(1)} fusion(bf16[512,1024]{1,0:T(8,128)(2,1)} %collective-permute-done.4, bf16[512,1024]{1,0:T(8,128)(2,1)S(1)} %collective-permute-done.10, pred[]{:T(512)S(6)} %eq.65), kind=kLoop, calls=%fused_computation.26 | loop fusion | flops 12582400 | bytes 2099201 | tf_op jit(solution)/shard_map/reduce_sum | solution.py:64
  138.5 4.1 %fusion.99 = (f32[512]{0:T(512)S(1)}, f32[512,800]{0,1:T(8,128)S(1)}) fusion(bf16[2048,800]{0,1:T(8,128)(2,1)S(1)} %collective-permute-done.6, f32[512]{0:T(512)S(1)} %add_rsqrt_fusion.2, f32[2048]{0:T(1024)S(1)} %convert_element_type.70, bf16[512,1024]{1,0:T(8,128)(2,1)} %collective-permute-done.2, bf16[512,1024]{1,0:T(8,128)(2,1)S(1)} %collective-permute-done.9, ...), kind=kOutput, calls=%fused_computation.227 | convolution fusion | flops 1691762176 | bytes 7024641 | tf_op jit(solution)/shard_map/dot_general | solution.py:69
  142.6 0.5 exponential_reduce_fusion.10
  143.1 5.5 %fusion.98 = (f32[512]{0:T(512)S(1)}, f32[512,1600]{0,1:T(8,128)S(1)}) fusion(bf16[2048,1600]{0,1:T(8,128)(2,1)S(1)} %constant_dynamic-update-slice_fusion.2, f32[512]{0:T(512)S(1)} %add_rsqrt_fusion.2, f32[2048]{0:T(1024)S(1)} %convert_element_type.70, bf16[512,1024]{1,0:T(8,128)(2,1)} %collective-permute-done.2, ...), kind=kOutput, calls=%fused_computation.226 | convolution fusion | flops 3369893376 | bytes 11939841 | tf_op jit(solution)/shard_map/dot_general | solution.py:69
  148.6 1.4 exponential_reduce_fusion.2
  150.0 4.3 %fusion.104 = (f32[512]{0:T(512)S(1)}, f32[512,800]{0,1:T(8,128)S(1)}) fusion(bf16[2048,800]{0,1:T(8,128)(2,1)S(1)} %collective-permute-done.6, f32[512]{0:T(512)S(1)} %add_rsqrt_fusion, f32[2048]{0:T(1024)S(1)} %convert_element_type.70, bf16[512,1024]{1,0:T(8,128)(2,1)} %collective-permute-done.4, bf16[512,1024]{1,0:T(8,128)(2,1)S(1)} %collective-permute-done.10, ...), kind=kOutput, calls=%fused_computation.232 | convolution fusion | flops 1691762176 | bytes 7024641 | tf_op jit(solution)/shard_map/dot_general | solution.py:69
  154.4 5.4 %fusion.107 = (f32[512]{0:T(512)S(1)}, f32[512,1600]{0,1:T(8,128)S(1)}) fusion(bf16[2048,1600]{0,1:T(8,128)(2,1)S(1)} %constant_dynamic-update-slice_fusion.2, f32[512]{0:T(512)S(1)} %add_rsqrt_fusion, f32[2048]{0:T(1024)S(1)} %convert_element_type.70, bf16[512,1024]{1,0:T(8,128)(2,1)} %collective-permute-done.4, ...), kind=kOutput, calls=%fused_computation.235 | convolution fusion | flops 3369893376 | bytes 11939841 | tf_op jit(solution)/shard_map/dot_general | solution.py:69
  159.8 1.3 collective-permute-done.12
  161.0 4.1 %fusion.100 = (f32[512]{0:T(512)S(1)}, f32[512,800]{0,1:T(8,128)S(1)}) fusion(bf16[2048,800]{0,1:T(8,128)(2,1)S(1)} %collective-permute-done.11, f32[2048]{0:T(1024)S(1)} %convert_element_type.70, f32[512]{0:T(512)S(1)} %add_rsqrt_fusion.3, bf16[512,1024]{1,0:T(8,128)(2,1)S(1)} %copy-done, bf16[512,1024]{1,0:T(8,128)(2,1)} %collective-permute-done, ...), kind=kOutput, calls=%fused_computation.228 | convolution fusion | flops 1691762176 | bytes 7024641 | tf_op jit(solution)/shard_map/dot_general | solution.py:69
  165.1 4.1 %fusion.101 = (f32[512]{0:T(512)S(1)}, f32[512,800]{0,1:T(8,128)S(1)}) fusion(bf16[2048,800]{0,1:T(8,128)(2,1)S(1)} %collective-permute-done.11, f32[512]{0:T(512)S(1)} %add_rsqrt_fusion.2, f32[2048]{0:T(1024)S(1)} %convert_element_type.70, bf16[512,1024]{1,0:T(8,128)(2,1)} %collective-permute-done.2, bf16[512,1024]{1,0:T(8,128)(2,1)S(1)} %collective-permute-done.9, ...), kind=kOutput, calls=%fused_computation.229 | convolution fusion | flops 1691762176 | bytes 7024641 | tf_op jit(solution)/shard_map/dot_general | solution.py:69
  169.2 4.3 %fusion.103 = (f32[512]{0:T(512)S(1)}, f32[512,800]{0,1:T(8,128)S(1)}) fusion(bf16[2048,800]{0,1:T(8,128)(2,1)S(1)} %collective-permute-done.11, f32[512]{0:T(512)S(1)} %add_rsqrt_fusion, f32[2048]{0:T(1024)S(1)} %convert_element_type.70, bf16[512,1024]{1,0:T(8,128)(2,1)} %collective-permute-done.4, bf16[512,1024]{1,0:T(8,128)(2,1)S(1)} %collective-permute-done.10, ...), kind=kOutput, calls=%fused_computation.231 | convolution fusion | flops 1691762176 | bytes 7024641 | tf_op jit(solution)/shard_map/dot_general | solution.py:69
  173.6 0.6 fusion.6
  174.2 2.1 fusion.102
  176.3 3.8 %fusion.106 = (f32[512]{0:T(512)S(1)}, f32[512,1600]{0,1:T(8,128)S(1)}) fusion(bf16[2048,1600]{0,1:T(8,128)(2,1)S(1)} %constant_dynamic-update-slice_fusion.2, f32[512]{0:T(512)S(1)} %add_rsqrt_fusion.1, f32[2048]{0:T(1024)S(1)} %convert_element_type.70, bf16[512,1024]{1,0:T(8,128)(2,1)S(1)} %collective-permute-done.7, ...), kind=kOutput, calls=%fused_computation.234 | convolution fusion | flops 3369893376 | bytes 11939841 | tf_op jit(solution)/shard_map/dot_general | solution.py:69
  180.2 2.1 fusion.105
  182.3 3.6 %exponential_reduce_fusion.9 = (f32[512]{0:T(512)S(1)}, f32[512]{0:T(512)S(1)}, f32[512]{0:T(512)S(1)}, f32[512]{0:T(512)S(1)}, f32[512]{0:T(512)S(1)}, /*index=...) fusion(f32[512,800]{0,1:T(8,128)S(1)} %get-tuple-element.158, ...), kind=kLoop, calls=%fused_computation.48 | loop fusion | flops 17193984 | bytes 9894144 | tf_op jit(solution)/shard_map/reduce_sum | solution.py:73
  186.0 2.6 %exponential_reduce_fusion.1 = (f32[512]{0:T(512)S(1)}, f32[512]{0:T(512)S(1)}, f32[512]{0:T(512)S(1)}, f32[512]{0:T(512)S(1)}, f32[512]{0:T(512)S(1)}, /*index=5*/f32[512]{0:T(512)S(1)}) fusion(f32[512,1600]{0,1:T(8,128)S(1)} %get-tuple-element.170, f32[512]{0:T(512)S(1)} %get-tuple-element.169, s32[512]{0:T(512)S(1)} %bitcast.266, ...), kind=kLoop, calls=%fused_computation.12 | loop fusion | flops 11465728 | bytes 6580480 | tf_op jit(solution)/shard_map/reduce_sum | solution.py:73
  189.2 0.6 gather_fusion
  189.9 0.6 reshape.319
  190.5 3.5 %all-to-all-start = ((f32[8,4,256]{2,1,0:T(4,128)}), f32[8,4,256]{2,1,0:T(4,128)S(1)}, u32[]{:S(2)}, u32[]{:S(2)}) async-start(f32[8,4,256]{2,1,0:T(4,128)} %reshape.319), calls=%async_computation | async-start | bytes 65536 | tf_op jit(solution)/shard_map/all_to_all | solution.py:159
  194.1 6.6 %all-to-all-done = f32[8,4,256]{2,1,0:T(4,128)S(1)} async-done(((f32[8,4,256]{2,1,0:T(4,128)}), f32[8,4,256]{2,1,0:T(4,128)S(1)}, u32[]{:S(2)}, u32[]{:S(2)}) %all-to-all-start) | async-done | bytes 32800 | tf_op jit(solution)/shard_map/all_to_all | solution.py:159
  201.1 8.9 %all_to_all.10 = f32[32,3,1]{1,2,0:T(1,128)S(1)} all-to-all(f32[32,3,1]{1,2,0:T(1,128)S(1)} %bitcast.255), channel_id=1, replica_groups=mesh['dh'=4,'p'=2,'dl'=2,'t'=2] {'dh','p','dl','t'}, dimensions={0} | all-to-all | bytes 768 | tf_op jit(solution)/shard_map/all_to_all | solution.py:182
  210.0 0.7 fusion.95
  (86 shorter events, 1.9 us)
Async XLA Ops:
  0.6 63.8 %collective-permute-start.1 = (bf16[2048,800]{0,1:T(8,128)(2,1)}, bf16[2048,800]{0,1:T(8,128)(2,1)S(1)}, u32[]{:S(2)}, u32[]{:S(2)}) collective-permute-start(bf16[2048,800]{0,1:T(8,128)(2,1)} %param.9), channel_id=1, source_target_pairs={{0,2},{2,0},{1,3},{3,1},{4,6},{6,4},{5,7},{7,5},{8,10},{10,8},{9,1... | collective-permute-start | bytes 9830408 | tf_op jit(solution)/shard_map/ppermute | solution.py:14
  1.1 60.3 %collective-permute-start = (bf16[512,1024]{1,0:T(8,128)(2,1)}, bf16[512,1024]{1,0:T(8,128)(2,1)}, u32[]{:S(2)}, u32[]{:S(2)}) collective-permute-start(bf16[512,1024]{1,0:T(8,128)(2,1)} %param.7), channel_id=1, source_target_pairs={{0,1},{1,0},{2,3},{3,2},{4,5},{5,4},{6,7},{7,6},{8,9},{9,8},{10,11... | collective-permute-start | bytes 3145736 | tf_op jit(solution)/shard_map/ppermute | solution.py:14
  3.7 58.4 %collective-permute-start.2 = (bf16[512,1024]{1,0:T(8,128)(2,1)}, bf16[512,1024]{1,0:T(8,128)(2,1)}, u32[]{:S(2)}, u32[]{:S(2)}) collective-permute-start(bf16[512,1024]{1,0:T(8,128)(2,1)} %param.7), channel_id=1, source_target_pairs={{0,8},{8,16},{16,24},{24,0},{1,9},{9,17},{17,25},{25,1},{2,10},{10... | collective-permute-start | bytes 3145736 | tf_op jit(solution)/shard_map/ppermute | solution.py:29
  5.3 59.1 %collective-permute-start.4 = (bf16[512,1024]{1,0:T(8,128)(2,1)}, bf16[512,1024]{1,0:T(8,128)(2,1)}, u32[]{:S(2)}, u32[]{:S(2)}) collective-permute-start(bf16[512,1024]{1,0:T(8,128)(2,1)} %param.7), channel_id=1, source_target_pairs={{0,24},{8,0},{16,8},{24,16},{1,25},{9,1},{17,9},{25,17},{2,26},{10... | collective-permute-start | bytes 3145736 | tf_op jit(solution)/shard_map/ppermute | solution.py:29
  8.2 45.4 %collective-permute-start.3 = (bf16[1,1024]{1,0:T(2,128)(2,1)S(1)}, bf16[1,1024]{1,0:T(2,128)(2,1)S(1)}, u32[]{:S(2)}, u32[]{:S(2)}) collective-permute-start(bf16[1,1024]{1,0:T(2,128)(2,1)S(1)} %constant_dynamic-update-slice_fusion), channel_id=1, source_target_pairs={{0,8},{8,16},{16,24},{24,0},{1,9},{9,17},{17,25},{25,1},{2,10},{10... | collective-permute-start | bytes 6152 | tf_op jit(solution)/shard_map/ppermute | solution.py:29
  53.7 3.6 %collective-permute-start.5 = (bf16[1,1024]{1,0:T(2,128)(2,1)S(1)}, bf16[1,1024]{1,0:T(2,128)(2,1)S(1)}, u32[]{:S(2)}, u32[]{:S(2)}) collective-permute-start(bf16[1,1024]{1,0:T(2,128)(2,1)S(1)} %constant_dynamic-update-slice_fusion), channel_id=1, source_target_pairs={{0,24},{8,0},{16,8},{24,16},{1,25},{9,1},{17,9},{25,17},{2,26},{10... | collective-permute-start | bytes 6152 | tf_op jit(solution)/shard_map/ppermute | solution.py:29
  57.3 71.0 %collective-permute-start.6 = (bf16[2048,800]{0,1:T(8,128)(2,1)}, bf16[2048,800]{0,1:T(8,128)(2,1)S(1)}, u32[]{:S(2)}, u32[]{:S(2)}) collective-permute-start(bf16[2048,800]{0,1:T(8,128)(2,1)} %param.9), channel_id=1, source_target_pairs={{0,4},{4,0},{1,5},{5,1},{2,6},{6,2},{3,7},{7,3},{8,12},{12,8},{9,1... | collective-permute-start | bytes 9830408 | tf_op jit(solution)/shard_map/ppermute | solution.py:14
  59.0 2.4 %copy-start = (bf16[512,1024]{1,0:T(8,128)(2,1)S(1)}, bf16[512,1024]{1,0:T(8,128)(2,1)}, u32[]{:S(2)}) copy-start(bf16[512,1024]{1,0:T(8,128)(2,1)} %param.7) | copy-start | bytes 3145732
  61.4 71.6 %collective-permute-start.7 = (bf16[512,1024]{1,0:T(8,128)(2,1)S(1)}, bf16[512,1024]{1,0:T(8,128)(2,1)S(1)}, u32[]{:S(2)}, u32[]{:S(2)}) collective-permute-start(bf16[512,1024]{1,0:T(8,128)(2,1)S(1)} %copy-done), channel_id=1, source_target_pairs={{0,16},{8,24},{16,0},{24,8},{1,17},{9,25},{17,1},{25,9},{2,18},{10... | collective-permute-start | bytes 3145736 | tf_op jit(solution)/shard_map/ppermute | solution.py:29
  62.2 70.8 %collective-permute-start.8 = (bf16[1,1024]{1,0:T(2,128)(2,1)S(1)}, bf16[1,1024]{1,0:T(2,128)(2,1)S(1)}, u32[]{:S(2)}, u32[]{:S(2)}) collective-permute-start(bf16[1,1024]{1,0:T(2,128)(2,1)S(1)} %constant_dynamic-update-slice_fusion), channel_id=1, source_target_pairs={{0,16},{8,24},{16,0},{24,8},{1,17},{9,25},{17,1},{25,9},{2,18},{10... | collective-permute-start | bytes 6152 | tf_op jit(solution)/shard_map/ppermute | solution.py:29
  64.4 68.6 %collective-permute-start.9 = (bf16[512,1024]{1,0:T(8,128)(2,1)}, bf16[512,1024]{1,0:T(8,128)(2,1)S(1)}, u32[]{:S(2)}, u32[]{:S(2)}) collective-permute-start(bf16[512,1024]{1,0:T(8,128)(2,1)} %collective-permute-done.2), channel_id=1, source_target_pairs={{0,1},{1,0},{2,3},{3,2},{4,5},{5,4},{6,7},{7,6},{8,9},{9,8},{10,11... | collective-permute-start | bytes 3145736 | tf_op jit(solution)/shard_map/ppermute | solution.py:14
  65.0 68.1 %collective-permute-start.10 = (bf16[512,1024]{1,0:T(8,128)(2,1)}, bf16[512,1024]{1,0:T(8,128)(2,1)S(1)}, u32[]{:S(2)}, u32[]{:S(2)}) collective-permute-start(bf16[512,1024]{1,0:T(8,128)(2,1)} %collective-permute-done.4), channel_id=1, source_target_pairs={{0,1},{1,0},{2,3},{3,2},{4,5},{5,4},{6,7},{7,6},{8,9},{9,8},{10,11... | collective-permute-start | bytes 3145736 | tf_op jit(solution)/shard_map/ppermute | solution.py:14
  69.0 5.4 %copy-start.1 = (s32[512]{0:T(512)S(1)}, s32[512]{0:T(512)}, u32[]{:S(2)}) copy-start(s32[512]{0:T(512)} %param.10) | copy-start | bytes 6148
  132.9 28.1 %collective-permute-start.11 = (bf16[2048,800]{0,1:T(8,128)(2,1)S(1)}, bf16[2048,800]{0,1:T(8,128)(2,1)S(1)}, u32[]{:S(2)}, u32[]{:S(2)}) collective-permute-start(bf16[2048,800]{0,1:T(8,128)(2,1)S(1)} %collective-permute-done.6), channel_id=1, source_target_pairs={{0,2},{2,0},{1,3},{3,1},{4,6},{6,4},{5,7},{7,5},{8,10},{10,8},{9,1... | collective-permute-start | bytes 9830408 | tf_op jit(solution)/shard_map/ppermute | solution.py:14
  135.4 25.6 %collective-permute-start.12 = (bf16[512,1024]{1,0:T(8,128)(2,1)S(1)}, bf16[512,1024]{1,0:T(8,128)(2,1)S(1)}, u32[]{:S(2)}, u32[]{:S(2)}) collective-permute-start(bf16[512,1024]{1,0:T(8,128)(2,1)S(1)} %collective-permute-done.7), channel_id=1, source_target_pairs={{0,1},{1,0},{2,3},{3,2},{4,5},{5,4},{6,7},{7,6},{8,9},{9,8},{10,11... | collective-permute-start | bytes 3145736 | tf_op jit(solution)/shard_map/ppermute | solution.py:14
  185.9 8.1 %copy-start.5 = (s32[16]{0:T(128)S(1)}, s32[16]{0:T(128)}, u32[]{:S(2)}) copy-start(s32[16]{0:T(128)} %param.13) | copy-start | bytes 196
  186.0 14.8 %copy-start.4 = (s32[512]{0:T(512)S(1)}, s32[512]{0:T(512)}, u32[]{:S(2)}) copy-start(s32[512]{0:T(512)} %param.11) | copy-start | bytes 6148
  190.5 10.2 %all-to-all-start = ((f32[8,4,256]{2,1,0:T(4,128)}), f32[8,4,256]{2,1,0:T(4,128)S(1)}, u32[]{:S(2)}, u32[]{:S(2)}) async-start(f32[8,4,256]{2,1,0:T(4,128)} %reshape.319), calls=%async_computation | async-start | bytes 65536 | tf_op jit(solution)/shard_map/all_to_all | solution.py:159
  200.9 11.8 %copy-start.3 = (f32[256]{0:T(256)}, f32[256]{0:T(256)S(1)}, u32[]{:S(2)}) copy-start(f32[256]{0:T(256)S(1)} %get-tuple-element.96) | copy-start | bytes 3076
  200.9 11.8 %copy-start.2 = (f32[256]{0:T(256)}, f32[256]{0:T(256)S(1)}, u32[]{:S(2)}) copy-start(f32[256]{0:T(256)S(1)} %subtract_multiply_fusion.1) | copy-start | bytes 3076
